TPU v7x, 512 devices: a whole 4x8x8 slice. The times are simulated.
512 devices in a mesh: frame: 8 (over y_lo, core), space: 64 (over x, y_hi, z).
Axes of the slice: x: 4, y: 8 (y_hi: 2, y_lo: 4; y = y_hi * 4 + y_lo), z: 8, core: 2. Of those that a mesh axis runs over, the one named last changes fastest.
Arguments:
- queries: bfloat16 [8, 960, 8, 1024], P('frame', 'space'), may hold values from -38 to 38
- key_proj: bfloat16 [8, 960, 8, 1024], P('frame', 'space'), may hold values from -6 to 6
- value_proj: bfloat16 [8, 960, 8, 1024], P('frame', 'space'), may hold values from -6 to 6
- grad_out: bfloat16 [8, 960, 8, 1024], P('frame', 'space'), may hold values from -12 to 12
- gate_vec: float32 [8, 1024], replicated, may hold values from 0.3 to 3
Outputs:
- grad_query: bfloat16 [8, 960, 8, 1024], P('frame', 'space')
- grad_key: bfloat16 [8, 960, 8, 1024], P('frame', 'space')
- grad_value: bfloat16 [8, 960, 8, 1024], P('frame', 'space')
- grad_gate: float32 [64, 128], P('space')
All inputs are finite; a program needn't handle non-finite values.
Results may differ from a plain program's by a relative error of at most 0.024.
Values may be sent and summed in bfloat16 or wider, within the bound.
No kernel may reach another device: no remote copies, remote signals or barrier semaphores. Data moves between devices by JAX's collectives and lax.ppermute only.
A program may use at most 64 MiB of HBM per device.

v0:
```python
import math

import jax
import jax.numpy as jnp
from jax import lax
from jax.sharding import PartitionSpec as P

DH = 128


def shortened(value):

    def short(part):
        return part.astype(jnp.bfloat16) if part.dtype == jnp.float32 else part

    return jax.tree.map(short, value)


def item_grads(query_one, key_one, value_one, upstream, gate_row):
    channels = query_one.shape[1]
    inv_root = 1.0 / math.sqrt(channels)
    scores = jnp.dot(query_one, key_one.T, preferred_element_type=jnp.float32) * inv_root
    row_peak = jnp.max(scores, axis=-1, keepdims=True)
    exp_terms = jnp.exp(scores - row_peak)
    attention = exp_terms / jnp.sum(exp_terms, axis=-1, keepdims=True)
    attention_low = attention.astype(jnp.bfloat16)
    attended_blk = jnp.dot(attention_low, value_one, preferred_element_type=jnp.float32)
    upstream_wide = upstream.astype(jnp.float32)
    cotangent = (gate_row[None, :] * upstream_wide).astype(jnp.bfloat16)
    gate_part = jnp.sum(upstream_wide * attended_blk, axis=0)
    grad_attn = jnp.dot(cotangent, value_one.T, preferred_element_type=jnp.float32)
    row_terms = jnp.sum(cotangent.astype(jnp.float32) * attended_blk, axis=-1, keepdims=True)
    grad_scores = (attention * (grad_attn - row_terms)).astype(jnp.bfloat16)
    query_parts = [
        (jnp.dot(grad_scores, key_one, preferred_element_type=jnp.float32) * inv_root).astype(
            jnp.bfloat16
        )
    ]
    attended_parts = [attended_blk]
    key_acc = jnp.dot(grad_scores.T, query_one, preferred_element_type=jnp.float32)
    value_acc = jnp.dot(attention_low.T, cotangent, preferred_element_type=jnp.float32)
    grad_query = jnp.concatenate(query_parts, axis=0)
    grad_key = (key_acc * inv_root).astype(jnp.bfloat16)
    grad_value = value_acc.astype(jnp.bfloat16)
    attended = jnp.concatenate(attended_parts, axis=0)
    return (grad_query, grad_key, grad_value, attended, gate_part)


def local(queries, key_proj, value_proj, grad_out, gate_vec):
    frames_local, pixels_local, clip_count, channels = queries.shape
    head_count = channels // DH
    pair_count = clip_count * head_count

    def by_pair(tensor):
        return tensor.reshape(frames_local, pixels_local, pair_count, DH)

    def by_width(tensor):
        return tensor.reshape(frames_local, pixels_local, clip_count, channels)

    query_all, key_all, value_all, upstream_all = (
        lax.all_to_all(by_pair(queries), "space", split_axis=2, concat_axis=1, tiled=True),
        lax.all_to_all(by_pair(key_proj), "space", split_axis=2, concat_axis=1, tiled=True),
        lax.all_to_all(by_pair(value_proj), "space", split_axis=2, concat_axis=1, tiled=True),
        lax.all_to_all(by_pair(grad_out), "space", split_axis=2, concat_axis=1, tiled=True),
    )
    pairs_local = query_all.shape[2]
    gate_rows = lax.dynamic_slice_in_dim(
        gate_vec.reshape(pair_count, DH), lax.axis_index("space") * pairs_local, pairs_local, 0
    )
    per_pair = jax.vmap(item_grads, in_axes=(1, 1, 1, 1, 0), out_axes=(1, 1, 1, 1, 0))
    per_frame = jax.vmap(per_pair, in_axes=(0, 0, 0, 0, None), out_axes=0)
    grad_query, grad_key, grad_value, attended, gate_parts = per_frame(
        query_all, key_all, value_all, upstream_all, gate_rows
    )
    back_query, back_key, back_value = (
        lax.all_to_all(
            shortened(grad_query), "space", split_axis=1, concat_axis=2, tiled=True
        ).astype(grad_query.dtype),
        lax.all_to_all(
            shortened(grad_key), "space", split_axis=1, concat_axis=2, tiled=True
        ).astype(grad_key.dtype),
        lax.all_to_all(
            shortened(grad_value), "space", split_axis=1, concat_axis=2, tiled=True
        ).astype(grad_value.dtype),
    )
    pair_terms = jnp.sum(gate_parts, axis=0)
    grad_gate = lax.psum(pair_terms, "frame")
    return (by_width(back_query), by_width(back_key), by_width(back_value), grad_gate)


def solution(mesh):
    in_specs = (
        P("frame", "space", None, None),
        P("frame", "space", None, None),
        P("frame", "space", None, None),
        P("frame", "space", None, None),
        P(),
    )
    out_specs = (
        P("frame", "space", None, None),
        P("frame", "space", None, None),
        P("frame", "space", None, None),
        P("space", None),
    )
    return jax.shard_map(local, mesh=mesh, in_specs=in_specs, out_specs=out_specs, check_vma=False)
```

profile of v0, /device:TPU:6, one launch (start us, length us, event | category | flops | bytes accessed | tf_op | source)
XLA Modules:
  0.0 185.2 jit_solution(16184186150969411239)
XLA Ops:
  0.7 1.1 reshape.151
  1.7 0.9 copy.34
  2.6 19.3 %all-to-all-start = ((bf16[1,15,64,128]{3,1,0,2:T(8,128)(2,1)}), bf16[1,15,64,128]{3,1,0,2:T(8,128)(2,1)S(1)}, u32[]{:S(2)}, u32[]{:S(2)}) async-start(bf16[1,15,64,128]{3,1,0,2:T(8,128)(2,1)} %copy.34), calls=%async_computation | async-start | bytes 524288 | tf_op jit(solution)/shard_map/all_to_all | solution.py:61
  21.9 1.1 reshape.153
  22.9 0.9 copy.35
  23.8 11.2 %all-to-all-done = bf16[1,15,64,128]{3,1,0,2:T(8,128)(2,1)S(1)} async-done(((bf16[1,15,64,128]{3,1,0,2:T(8,128)(2,1)}), bf16[1,15,64,128]{3,1,0,2:T(8,128)(2,1)S(1)}, u32[]{:S(2)}, u32[]{:S(2)}) %all-to-all-start) | async-done | bytes 245792 | tf_op jit(solution)/shard_map/all_to_all | solution.py:61
  35.0 8.9 %all-to-all-start.1 = ((bf16[1,15,64,128]{3,1,0,2:T(8,128)(2,1)}), bf16[1,15,64,128]{3,1,0,2:T(8,128)(2,1)S(1)}, u32[]{:S(2)}, u32[]{:S(2)}) async-start(bf16[1,15,64,128]{3,1,0,2:T(8,128)(2,1)} %copy.35), calls=%async_computation.1 | async-start | bytes 524288 | tf_op jit(solution)/shard_map/all_to_all | solution.py:62
  43.9 1.1 reshape.157
  45.0 0.9 copy.37
  45.8 12.3 %all-to-all-done.1 = bf16[1,15,64,128]{3,1,0,2:T(8,128)(2,1)S(1)} async-done(((bf16[1,15,64,128]{3,1,0,2:T(8,128)(2,1)}), bf16[1,15,64,128]{3,1,0,2:T(8,128)(2,1)S(1)}, u32[]{:S(2)}, u32[]{:S(2)}) %all-to-all-start.1) | async-done | bytes 245792 | tf_op jit(solution)/shard_map/all_to_all | solution.py:62
  58.1 7.6 %all-to-all-start.3 = ((bf16[1,15,64,128]{3,1,0,2:T(8,128)(2,1)}), bf16[1,15,64,128]{3,1,0,2:T(8,128)(2,1)S(1)}, u32[]{:S(2)}, u32[]{:S(2)}) async-start(bf16[1,15,64,128]{3,1,0,2:T(8,128)(2,1)} %copy.37), calls=%async_computation.3 | async-start | bytes 524288 | tf_op jit(solution)/shard_map/all_to_all | solution.py:63
  65.8 0.1 reshape.156
  65.9 0.9 copy.36
  66.8 13.3 %all-to-all-done.3 = bf16[1,15,64,128]{3,1,0,2:T(8,128)(2,1)S(1)} async-done(((bf16[1,15,64,128]{3,1,0,2:T(8,128)(2,1)}), bf16[1,15,64,128]{3,1,0,2:T(8,128)(2,1)S(1)}, u32[]{:S(2)}, u32[]{:S(2)}) %all-to-all-start.3) | async-done | bytes 245792 | tf_op jit(solution)/shard_map/all_to_all | solution.py:63
  80.0 7.7 %all-to-all-start.2 = ((bf16[1,15,64,128]{3,1,0,2:T(8,128)(2,1)}), bf16[1,15,64,128]{3,1,0,2:T(8,128)(2,1)S(1)}, u32[]{:S(2)}, u32[]{:S(2)}) async-start(bf16[1,15,64,128]{3,1,0,2:T(8,128)(2,1)} %copy.36), calls=%async_computation.2 | async-start | bytes 524288 | tf_op jit(solution)/shard_map/all_to_all | solution.py:64
  87.7 0.1 reshape.160
  87.8 0.1 all_to_all.83
  87.9 0.1 reshape.159
  88.0 0.1 all_to_all.88
  88.1 0.1 reshape.152
  88.2 12.6 %all-to-all-done.2 = bf16[1,15,64,128]{3,1,0,2:T(8,128)(2,1)S(1)} async-done(((bf16[1,15,64,128]{3,1,0,2:T(8,128)(2,1)}), bf16[1,15,64,128]{3,1,0,2:T(8,128)(2,1)S(1)}, u32[]{:S(2)}, u32[]{:S(2)}) %all-to-all-start.2) | async-done | bytes 245792 | tf_op jit(solution)/shard_map/all_to_all | solution.py:64
  100.8 0.1 fusion.11
  100.9 0.8 convert_element_type.71
  101.8 0.7 multiply_reduce_fusion
  102.5 0.7 fusion.1
  103.2 1.2 multiply_reduce_fusion.1
  104.3 0.0 copy-done
  104.3 0.1 copy-done.2
  104.4 1.1 multiply_convert_fusion
  105.5 0.8 fusion.5
  106.3 0.4 copy.54
  106.7 0.5 broadcast.35
  107.2 2.1 %reduce.14 = bf16[960,128]{1,0:T(8,128)(2,1)S(1)} reduce(bf16[960,1,1,128]{3,2,1,0:T(2,128)(2,1)S(1)} %bitcast.101, bf16[]{:T(256)} %broadcast.35), dimensions={1,2}, to_apply=%bitcast.96.reduce_sub_computation | reduce | bytes 491522
  109.3 0.9 reshape.170
  110.2 7.7 %all-to-all-start.4 = ((bf16[64,2,960]{2,1,0:T(2,128)(2,1)}), bf16[64,2,960]{2,1,0:T(2,128)(2,1)S(1)}, u32[]{:S(2)}, u32[]{:S(2)}) async-start(bf16[64,2,960]{2,1,0:T(2,128)(2,1)} %reshape.170), calls=%async_computation.4 | async-start | bytes 524288 | tf_op jit(solution)/shard_map/all_to_all | solution.py:76
  117.9 0.7 fusion.4
  118.6 0.4 copy.53
  119.0 2.1 %reduce.15 = bf16[960,128]{1,0:T(8,128)(2,1)S(1)} reduce(bf16[960,1,1,128]{3,2,1,0:T(2,128)(2,1)S(1)} %bitcast.103, bf16[]{:T(256)} %broadcast.35), dimensions={1,2}, to_apply=%bitcast.95.reduce_sub_computation | reduce | bytes 491522
  121.1 0.9 reshape.172
  122.0 9.1 %all-to-all-done.4 = bf16[64,2,960]{2,1,0:T(2,128)(2,1)S(1)} async-done(((bf16[64,2,960]{2,1,0:T(2,128)(2,1)}), bf16[64,2,960]{2,1,0:T(2,128)(2,1)S(1)}, u32[]{:S(2)}, u32[]{:S(2)}) %all-to-all-start.4) | async-done | bytes 245792 | tf_op jit(solution)/shard_map/all_to_all | solution.py:76
  131.1 7.9 %all-to-all-start.5 = ((bf16[64,2,960]{2,1,0:T(2,128)(2,1)}), bf16[64,2,960]{2,1,0:T(2,128)(2,1)S(1)}, u32[]{:S(2)}, u32[]{:S(2)}) async-start(bf16[64,2,960]{2,1,0:T(2,128)(2,1)} %reshape.172), calls=%async_computation.5 | async-start | bytes 524288 | tf_op jit(solution)/shard_map/all_to_all | solution.py:79
  139.0 3.0 %fusion.6 = bf16[1,960,1,128]{3,1,2,0:T(8,128)(2,1)S(1)} fusion(f32[960,128]{1,0:T(8,128)S(1)} %reshape.164, f32[128]{0:T(128)S(1)} %dynamic-slice_bitcast_fusion, f32[960,960]{0,1:T(8,128)} %copy-done, f32[960]{0:T(1024)S(1)} %fusion.1, f32[960]{0:T(1024)S(1)} %get-tuple-element.6), kind=kOutput, calls=%fused_computation.12 | convolution fusion | flops 239984640 | bytes 4431872 | tf_op jit(solution)/shard_map/vmap(vmap())/dot_general | solution.py:41
  142.0 0.4 copy.52
  142.4 2.1 %reduce.16 = bf16[960,128]{1,0:T(8,128)(2,1)S(1)} reduce(bf16[960,1,1,128]{3,2,1,0:T(2,128)(2,1)S(1)} %bitcast.102, bf16[]{:T(256)} %broadcast.35), dimensions={1,2}, to_apply=%bitcast.94.reduce_sub_computation | reduce | bytes 491522
  144.5 0.9 reshape.174
  145.5 6.7 %all-to-all-done.5 = bf16[64,2,960]{2,1,0:T(2,128)(2,1)S(1)} async-done(((bf16[64,2,960]{2,1,0:T(2,128)(2,1)}), bf16[64,2,960]{2,1,0:T(2,128)(2,1)S(1)}, u32[]{:S(2)}, u32[]{:S(2)}) %all-to-all-start.5) | async-done | bytes 245792 | tf_op jit(solution)/shard_map/all_to_all | solution.py:79
  152.2 8.4 %all-to-all-start.6 = ((bf16[64,2,960]{2,1,0:T(2,128)(2,1)}), bf16[64,2,960]{2,1,0:T(2,128)(2,1)S(1)}, u32[]{:S(2)}, u32[]{:S(2)}) async-start(bf16[64,2,960]{2,1,0:T(2,128)(2,1)} %reshape.174), calls=%async_computation.6 | async-start | bytes 524288 | tf_op jit(solution)/shard_map/all_to_all | solution.py:82
  160.6 16.3 %psum.7 = f32[1,128]{1,0:T(1,128)} all-reduce(f32[1,128]{1,0:T(1,128)S(1)} %bitcast.108), channel_id=1, replica_groups=mesh['frame'=8,'space'=64] {'frame'}, use_global_device_ids=true, to_apply=%region_4.0 | all-reduce | flops 128 | bytes 1024 | tf_op jit(solution)/shard_map/psum | solution.py:87
  176.9 0.4 reshape.171
  177.3 1.4 bitcast_reduce_fusion.2
  178.7 0.1 all_to_all.90
  178.8 0.1 copy.40
  178.9 0.8 reshape.161
  179.7 0.4 reshape.173
  180.0 1.4 bitcast_reduce_fusion.1
  181.5 0.1 all_to_all.93
  181.6 0.1 copy.42
  181.6 0.8 reshape.162
  182.4 0.0 all-to-all-done.6
  182.4 0.4 reshape.175
  182.8 1.4 bitcast_reduce_fusion
  184.2 0.1 all_to_all.96
  184.3 0.1 copy.44
  184.4 0.8 reshape.163
  (10 shorter events, 0.1 us)
Async XLA Ops:
  0.6 65.1 %copy-start.1 = (bf16[1,15,8,1024]{3,2,1,0:T(8,128)(2,1)S(1)}, bf16[1,15,8,1024]{3,2,1,0:T(8,128)(2,1)}, u32[]{:S(2)}) copy-start(bf16[1,15,8,1024]{3,2,1,0:T(8,128)(2,1)} %param.8) | copy-start | bytes 737284
  0.6 87.0 %copy-start.3 = (f32[8,1024]{1,0:T(8,128)S(1)}, f32[8,1024]{1,0:T(8,128)}, u32[]{:S(2)}) copy-start(f32[8,1024]{1,0:T(8,128)} %param.9) | copy-start | bytes 98308
  2.6 32.4 %all-to-all-start = ((bf16[1,15,64,128]{3,1,0,2:T(8,128)(2,1)}), bf16[1,15,64,128]{3,1,0,2:T(8,128)(2,1)S(1)}, u32[]{:S(2)}, u32[]{:S(2)}) async-start(bf16[1,15,64,128]{3,1,0,2:T(8,128)(2,1)} %copy.34), calls=%async_computation | async-start | bytes 524288 | tf_op jit(solution)/shard_map/all_to_all | solution.py:61
  35.0 23.1 %all-to-all-start.1 = ((bf16[1,15,64,128]{3,1,0,2:T(8,128)(2,1)}), bf16[1,15,64,128]{3,1,0,2:T(8,128)(2,1)S(1)}, u32[]{:S(2)}, u32[]{:S(2)}) async-start(bf16[1,15,64,128]{3,1,0,2:T(8,128)(2,1)} %copy.35), calls=%async_computation.1 | async-start | bytes 524288 | tf_op jit(solution)/shard_map/all_to_all | solution.py:62
  58.1 21.9 %all-to-all-start.3 = ((bf16[1,15,64,128]{3,1,0,2:T(8,128)(2,1)}), bf16[1,15,64,128]{3,1,0,2:T(8,128)(2,1)S(1)}, u32[]{:S(2)}, u32[]{:S(2)}) async-start(bf16[1,15,64,128]{3,1,0,2:T(8,128)(2,1)} %copy.37), calls=%async_computation.3 | async-start | bytes 524288 | tf_op jit(solution)/shard_map/all_to_all | solution.py:63
  80.0 20.8 %all-to-all-start.2 = ((bf16[1,15,64,128]{3,1,0,2:T(8,128)(2,1)}), bf16[1,15,64,128]{3,1,0,2:T(8,128)(2,1)S(1)}, u32[]{:S(2)}, u32[]{:S(2)}) async-start(bf16[1,15,64,128]{3,1,0,2:T(8,128)(2,1)} %copy.36), calls=%async_computation.2 | async-start | bytes 524288 | tf_op jit(solution)/shard_map/all_to_all | solution.py:64
  102.5 1.9 %copy-start = (f32[960,960]{0,1:T(8,128)}, f32[960,960]{0,1:T(8,128)S(1)}, u32[]{:S(2)}) copy-start(f32[960,960]{0,1:T(8,128)S(1)} %get-tuple-element.7) | copy-start | bytes 11059204
  103.2 1.2 copy-start.2
  110.2 20.9 %all-to-all-start.4 = ((bf16[64,2,960]{2,1,0:T(2,128)(2,1)}), bf16[64,2,960]{2,1,0:T(2,128)(2,1)S(1)}, u32[]{:S(2)}, u32[]{:S(2)}) async-start(bf16[64,2,960]{2,1,0:T(2,128)(2,1)} %reshape.170), calls=%async_computation.4 | async-start | bytes 524288 | tf_op jit(solution)/shard_map/all_to_all | solution.py:76
  131.1 21.1 %all-to-all-start.5 = ((bf16[64,2,960]{2,1,0:T(2,128)(2,1)}), bf16[64,2,960]{2,1,0:T(2,128)(2,1)S(1)}, u32[]{:S(2)}, u32[]{:S(2)}) async-start(bf16[64,2,960]{2,1,0:T(2,128)(2,1)} %reshape.172), calls=%async_computation.5 | async-start | bytes 524288 | tf_op jit(solution)/shard_map/all_to_all | solution.py:79
  152.2 30.2 %all-to-all-start.6 = ((bf16[64,2,960]{2,1,0:T(2,128)(2,1)}), bf16[64,2,960]{2,1,0:T(2,128)(2,1)S(1)}, u32[]{:S(2)}, u32[]{:S(2)}) async-start(bf16[64,2,960]{2,1,0:T(2,128)(2,1)} %reshape.174), calls=%async_computation.6 | async-start | bytes 524288 | tf_op jit(solution)/shard_map/all_to_all | solution.py:82
where the time goes:
time: 186 us; the launch traced here: 185 us
  starting transfers between devices  67.5 us (36%)
  waiting for transfers between devices  65.2 us (35%)
  local copies, waits for them, and re-layouts  20.6 us (11%)
  blocking collectives  16.3 us (9%)
  matrix products  7.42 us (4%)
  other arithmetic  7.11 us (4%)
    all_to_all x1, starting transfers between devices, local(): lax.all_to_all(by_pair(queries), 'space', split_axis=2, concat_axis=1, ti...  19.3 us
    psum x1, blocking collectives, local(): grad_gate = lax.psum(pair_terms, 'frame')  16.3 us
    all_to_all x1, waiting for transfers between devices, local(): lax.all_to_all(by_pair(value_proj), 'space', split_axis=2, concat_axis=1,...  13.3 us
    all_to_all x1, waiting for transfers between devices, local(): lax.all_to_all(by_pair(grad_out), 'space', split_axis=2, concat_axis=1, t...  12.6 us
    all_to_all x1, waiting for transfers between devices, local(): lax.all_to_all(by_pair(key_proj), 'space', split_axis=2, concat_axis=1, t...  12.3 us
    all_to_all x1, waiting for transfers between devices, local(): lax.all_to_all(by_pair(queries), 'space', split_axis=2, concat_axis=1, ti...  11.2 us
    all_to_all x1, waiting for transfers between devices, local(): lax.all_to_all(shortened(grad_query), 'space', split_axis=1, concat_axis=...  9.06 us
    all_to_all x1, starting transfers between devices, local(): lax.all_to_all(by_pair(key_proj), 'space', split_axis=2, concat_axis=1, t...  8.88 us
  transfers between devices with their start and end apart: 7, of which 6 were waited for; matrix products, arithmetic and copies ran while one was open for 11% of the time, Pallas kernels for 0%

commit v1 on v0

--- a/solution.py
+++ b/solution.py
@@ -57,11 +57,12 @@
     def by_width(tensor):
         return tensor.reshape(frames_local, pixels_local, clip_count, channels)
 
+    stacked = jnp.stack(
+        [by_pair(queries), by_pair(key_proj), by_pair(value_proj), by_pair(grad_out)], axis=0
+    )
+    gathered = lax.all_to_all(stacked, "space", split_axis=3, concat_axis=2, tiled=True)
     query_all, key_all, value_all, upstream_all = (
-        lax.all_to_all(by_pair(queries), "space", split_axis=2, concat_axis=1, tiled=True),
-        lax.all_to_all(by_pair(key_proj), "space", split_axis=2, concat_axis=1, tiled=True),
-        lax.all_to_all(by_pair(value_proj), "space", split_axis=2, concat_axis=1, tiled=True),
-        lax.all_to_all(by_pair(grad_out), "space", split_axis=2, concat_axis=1, tiled=True),
+        gathered[0], gathered[1], gathered[2], gathered[3]
     )
     pairs_local = query_all.shape[2]
     gate_rows = lax.dynamic_slice_in_dim(
@@ -72,17 +73,9 @@
     grad_query, grad_key, grad_value, attended, gate_parts = per_frame(
         query_all, key_all, value_all, upstream_all, gate_rows
     )
-    back_query, back_key, back_value = (
-        lax.all_to_all(
-            shortened(grad_query), "space", split_axis=1, concat_axis=2, tiled=True
-        ).astype(grad_query.dtype),
-        lax.all_to_all(
-            shortened(grad_key), "space", split_axis=1, concat_axis=2, tiled=True
-        ).astype(grad_key.dtype),
-        lax.all_to_all(
-            shortened(grad_value), "space", split_axis=1, concat_axis=2, tiled=True
-        ).astype(grad_value.dtype),
-    )
+    grads = jnp.stack([grad_query, grad_key, grad_value], axis=0)
+    back = lax.all_to_all(grads, "space", split_axis=2, concat_axis=3, tiled=True)
+    back_query, back_key, back_value = back[0], back[1], back[2]
     pair_terms = jnp.sum(gate_parts, axis=0)
     grad_gate = lax.psum(pair_terms, "frame")
     return (by_width(back_query), by_width(back_key), by_width(back_value), grad_gate)

time: 186 us -> 114 us (0.61)
  waiting for transfers between devices: 65.2 us -> 26.3 us
  starting transfers between devices: 67.5 us -> 30.4 us
  blocking collectives: 16.3 us -> 33.3 us
  local copies, waits for them, and re-layouts: 20.6 us -> 11 us
  matrix products: 7.42 us -> 5.31 us
    all_to_all x7 -> x2, waiting for transfers between devices: 65.2 us -> 26.3 us  [the longest x1 26.3 us: local(): lax.all_to_all(stacked, 'space', split_axis=3, concat_axis=2, tiled=True)]
    all_to_all x7 -> x2, starting transfers between devices: 67.5 us -> 30.4 us  [the longest x1 19.3 us: local(): lax.all_to_all(stacked, 'space', split_axis=3, concat_axis=2, tiled=True)]
    psum x1, blocking collectives: 16.3 us -> 33.3 us  [local(): grad_gate = lax.psum(pair_terms, 'frame')]
    another operation x2 -> x12, local copies, waits for them, and re-layouts: 0.18 us -> 10.2 us  [the longest x5 5.93 us: local(): jnp.stack([by_pair(queries), by_pair(key_proj), by_pair(value_proj), by_p...]
    reshape x12 -> x0, local copies, waits for them, and re-layouts: 9.25 us -> none  [the longest x8 6.75 us: by_pair(): return tensor.reshape(frames_local, pixels_local, pair_count, DH)]
    unnamed x3 -> x0, other arithmetic: 6.33 us -> none
    slice x0 -> x1, other arithmetic: none -> 5.58 us  [local(): gathered[2]]
    all_to_all x11 -> x1, local copies, waits for them, and re-layouts: 4.86 us -> 0.14 us  [local(): lax.all_to_all(grads, 'space', split_axis=2, concat_axis=3, tiled=True)]
  transfers between devices with their start and end apart: 7 -> 2, of which waited for: 6 -> 1; matrix products, arithmetic and copies ran while one was open for 11% -> 0% of each run, Pallas kernels for 0% -> 0%
where the time goes in v1:
time: 114 us
  blocking collectives  33.3 us (29%)
  starting transfers between devices  30.4 us (27%)
  waiting for transfers between devices  26.3 us (23%)
  local copies, waits for them, and re-layouts  11 us (10%)
  other arithmetic  6.48 us (6%)
  matrix products  5.31 us (5%)
    psum x1, blocking collectives, local(): grad_gate = lax.psum(pair_terms, 'frame')  33.3 us
    all_to_all x1, waiting for transfers between devices, local(): lax.all_to_all(stacked, 'space', split_axis=3, concat_axis=2, tiled=True)  26.3 us
    all_to_all x1, starting transfers between devices, local(): lax.all_to_all(stacked, 'space', split_axis=3, concat_axis=2, tiled=True)  19.3 us
    all_to_all x1, starting transfers between devices, local(): lax.all_to_all(grads, 'space', split_axis=2, concat_axis=3, tiled=True)  11.1 us
    another operation x5, local copies, waits for them, and re-layouts, local(): jnp.stack([by_pair(queries), by_pair(key_proj), by_pair(value_proj), by_p...  5.93 us
    slice x1, other arithmetic, local(): gathered[2]  5.58 us
    another operation x3, local copies, waits for them, and re-layouts, by_width(): return tensor.reshape(frames_local, pixels_local, clip_count, channels)  2.4 us
  transfers between devices with their start and end apart: 2, of which 1 were waited for; matrix products, arithmetic and copies ran while one was open for 0% of the time, Pallas kernels for 0%

profile of v1, /device:TPU:6, one launch (start us, length us, event | category | flops | bytes accessed | tf_op | source)
XLA Modules:
  0.0 113.6 jit_solution(13844499719459496578)
XLA Ops:
  0.6 0.0 copy-start
  0.6 1.1 stack_reshape.12
  1.7 1.1 stack_reshape.13
  2.8 1.1 stack_reshape.14
  3.8 1.1 stack_reshape.15
  4.9 0.1 pad_maximum_fusion
  5.0 1.7 %copy.43 = bf16[4,1,15,64,128]{4,0,2,1,3:T(4,128)(2,1)} copy(bf16[4,1,15,64,128]{4,3,2,1,0:T(8,128)(2,1)S(1)} %pad_maximum_fusion) | data formatting | bytes 1966080 | tf_op jit(solution)/shard_map/stack | solution.py:60
  6.7 19.3 %all-to-all-start = ((bf16[4,1,15,64,128]{4,0,2,1,3:T(4,128)(2,1)}), bf16[4,1,15,64,128]{4,0,2,1,3:T(4,128)(2,1)S(1)}, u32[]{:S(2)}, u32[]{:S(2)}) async-start(bf16[4,1,15,64,128]{4,0,2,1,3:T(4,128)(2,1)} %copy.43), calls=%async_computation | async-start | bytes 1966080 | tf_op jit(solution)/shard_map/all_to_all | solution.py:63
  26.0 0.0 copy-done
  26.1 26.3 %all-to-all-done = bf16[4,1,15,64,128]{4,0,2,1,3:T(4,128)(2,1)S(1)} async-done(((bf16[4,1,15,64,128]{4,0,2,1,3:T(4,128)(2,1)}), bf16[4,1,15,64,128]{4,0,2,1,3:T(4,128)(2,1)S(1)}, u32[]{:S(2)}, u32[]{:S(2)}) %all-to-all-start) | async-done | bytes 983072 | tf_op jit(solution)/shard_map/all_to_all | solution.py:63
  52.3 5.6 %slice_reduce_fusion = (bf16[64,15,128]{2,1,0:T(8,128)(2,1)S(1)}, bf16[64,15,128]{2,1,0:T(8,128)(2,1)S(1)}, bf16[64,15,128]{2,1,0:T(8,128)(2,1)S(1)}, bf16[64,15...) fusion(bf16[4,1,64,15,1,128]{5,0,3,2,4,1:T(4,128)(2,1)S(1)} %bitcast.56, f32[128]{0:T(128)S(1)} %dynamic-slice_bitcast_fusion), kind=kLoop, calls=%fused_computation.19 | loop fusion | flops 368640 | bytes 2458112 | tf_op jit(solution)/shard_map/slice | solution.py:65
  57.9 0.1 reshape.141
  58.0 0.1 squeeze.9
  58.1 0.1 reshape.142
  58.2 0.1 squeeze.8
  58.3 0.1 convert_element_type.58
  58.4 0.1 reshape.137
  58.5 0.7 multiply_reduce_fusion
  59.2 0.7 fusion.1
  59.9 0.9 fusion.6
  60.8 1.2 %multiply_reduce_fusion.1 = (f32[128]{0:T(128)S(1)}, f32[960]{0:T(1024)S(1)}) fusion(f32[960,128]{1,0:T(8,128)S(1)} %bitcast.60, f32[128]{0:T(128)S(1)} %dynamic-slice_bitcast_fusion, bf16[960,128]{1,0:T(8,128)(2,1)S(1)} %reshape.141, f32[960]{0:T(1024)S(1)} %fusion.1, f32[960]{0:T(1024)S(1)} %get-tuple-element.14, f32[960,960]{0,1:T(8,128)S(1)} %get-tuple-element.15), kind=kOutput, calls=%fused_computation.23 | convolution fusion | flops 240475072 | bytes 4436224 | tf_op jit(solution)/shard_map/vmap(vmap())/dot_general | solution.py:27
  61.9 1.1 multiply_convert_fusion
  63.1 0.7 fusion.4
  63.7 0.8 fusion.5
  64.5 0.1 pad_maximum_fusion.1
  64.6 1.6 %copy.45 = bf16[3,1,960,1,128]{4,0,3,1,2:T(4,128)(2,1)} copy(bf16[3,1,960,1,128]{4,2,3,1,0:T(8,128)(2,1)S(1)} %pad_maximum_fusion.1) | data formatting | bytes 1474560 | tf_op jit(solution)/shard_map/stack | solution.py:76
  66.2 11.1 %all-to-all-start.1 = ((bf16[3,1,960,1,128]{4,0,3,1,2:T(4,128)(2,1)}), bf16[3,1,960,1,128]{4,0,3,1,2:T(4,128)(2,1)S(1)}, u32[]{:S(2)}, u32[]{:S(2)}) async-start(bf16[3,1,960,1,128]{4,0,3,1,2:T(4,128)(2,1)} %copy.45), calls=%async_computation.1 | async-start | bytes 1966080 | tf_op jit(solution)/shard_map/all_to_all | solution.py:77
  77.4 33.3 %psum.7 = f32[1,128]{1,0:T(1,128)} all-reduce(f32[1,128]{1,0:T(1,128)S(1)} %bitcast.61), channel_id=1, replica_groups=mesh['frame'=8,'space'=64] {'frame'}, use_global_device_ids=true, to_apply=%region_4.0 | all-reduce | flops 128 | bytes 1024 | tf_op jit(solution)/shard_map/psum | solution.py:80
  110.7 0.0 all-to-all-done.1
  110.7 0.1 copy.59
  110.8 0.1 fusion.15
  111.0 0.1 copy.49
  111.1 0.8 reshape_squeeze.11
  111.9 0.1 copy.48
  111.9 0.8 reshape_squeeze.10
  112.7 0.1 copy.47
  112.8 0.8 reshape_squeeze.9
  (2 shorter events, 0.0 us)
Async XLA Ops:
  0.6 25.4 %copy-start = (f32[8,1024]{1,0:T(8,128)S(1)}, f32[8,1024]{1,0:T(8,128)}, u32[]{:S(2)}) copy-start(f32[8,1024]{1,0:T(8,128)} %param.9) | copy-start | bytes 98308
  6.7 45.6 %all-to-all-start = ((bf16[4,1,15,64,128]{4,0,2,1,3:T(4,128)(2,1)}), bf16[4,1,15,64,128]{4,0,2,1,3:T(4,128)(2,1)S(1)}, u32[]{:S(2)}, u32[]{:S(2)}) async-start(bf16[4,1,15,64,128]{4,0,2,1,3:T(4,128)(2,1)} %copy.43), calls=%async_computation | async-start | bytes 1966080 | tf_op jit(solution)/shard_map/all_to_all | solution.py:63
  66.2 44.5 %all-to-all-start.1 = ((bf16[3,1,960,1,128]{4,0,3,1,2:T(4,128)(2,1)}), bf16[3,1,960,1,128]{4,0,3,1,2:T(4,128)(2,1)S(1)}, u32[]{:S(2)}, u32[]{:S(2)}) async-start(bf16[3,1,960,1,128]{4,0,3,1,2:T(4,128)(2,1)} %copy.45), calls=%async_computation.1 | async-start | bytes 1966080 | tf_op jit(solution)/shard_map/all_to_all | solution.py:77

commit v2 on v1

--- a/solution.py
+++ b/solution.py
@@ -57,14 +57,14 @@
     def by_width(tensor):
         return tensor.reshape(frames_local, pixels_local, clip_count, channels)
 
-    stacked = jnp.stack(
-        [by_pair(queries), by_pair(key_proj), by_pair(value_proj), by_pair(grad_out)], axis=0
+    space_size = lax.axis_size("space")
+    pairs_local = pair_count // space_size
+    stacked = jnp.stack([by_pair(queries), by_pair(key_proj), by_pair(value_proj), by_pair(grad_out)], axis=3)
+    stacked = jnp.transpose(stacked, (2, 0, 1, 3, 4))
+    gathered = lax.all_to_all(stacked, "space", split_axis=0, concat_axis=2, tiled=True)
+    query_all, key_all, value_all, upstream_all = (
+        jnp.transpose(gathered[:, :, :, part, :], (1, 2, 0, 3)) for part in range(4)
     )
-    gathered = lax.all_to_all(stacked, "space", split_axis=3, concat_axis=2, tiled=True)
-    query_all, key_all, value_all, upstream_all = (
-        gathered[0], gathered[1], gathered[2], gathered[3]
-    )
-    pairs_local = query_all.shape[2]
     gate_rows = lax.dynamic_slice_in_dim(
         gate_vec.reshape(pair_count, DH), lax.axis_index("space") * pairs_local, pairs_local, 0
     )
@@ -73,9 +73,14 @@
     grad_query, grad_key, grad_value, attended, gate_parts = per_frame(
         query_all, key_all, value_all, upstream_all, gate_rows
     )
-    grads = jnp.stack([grad_query, grad_key, grad_value], axis=0)
-    back = lax.all_to_all(grads, "space", split_axis=2, concat_axis=3, tiled=True)
-    back_query, back_key, back_value = back[0], back[1], back[2]
+    grads = jnp.stack([grad_query, grad_key, grad_value], axis=3)
+    grads = jnp.transpose(grads, (2, 0, 1, 3, 4))
+    grads = grads.reshape(pairs_local, frames_local, space_size, pixels_local * 3, DH)
+    back = lax.all_to_all(grads, "space", split_axis=2, concat_axis=0, tiled=True)
+    back = back.reshape(pair_count, frames_local, pixels_local, 3, DH)
+    back_query, back_key, back_value = (
+        jnp.transpose(back[:, :, :, part, :], (1, 2, 0, 3)) for part in range(3)
+    )
     pair_terms = jnp.sum(gate_parts, axis=0)
     grad_gate = lax.psum(pair_terms, "frame")
     return (by_width(back_query), by_width(back_key), by_width(back_value), grad_gate)

time: 114 us -> 105 us (0.921)
  other arithmetic: 6.48 us -> 0.9 us
  blocking collectives: 33.3 us -> 29.1 us
    slice x1 -> x0, other arithmetic: 5.58 us -> none  [local(): gathered[2]]
    psum x1, blocking collectives: 33.3 us -> 29.1 us  [local(): grad_gate = lax.psum(pair_terms, 'frame')]
    reshape x0 -> x3, local copies, waits for them, and re-layouts: none -> 2.4 us  [by_width(): return tensor.reshape(frames_local, pixels_local, clip_count, channels)]
    another operation x7 -> x2, local copies, waits for them, and re-layouts: 4.26 us -> 1.98 us  [the longest x1 1.34 us: local(): grads.reshape(pairs_local, frames_local, space_size, pixels_local * 3, DH)]
    transpose x0 -> x2, local copies, waits for them, and re-layouts: none -> 1.76 us  [the longest x1 1.71 us: local(): stacked = jnp.transpose(stacked, (2, 0, 1, 3, 4))]
    another operation x5 -> x4, local copies, waits for them, and re-layouts: 5.93 us -> 4.22 us  [local(): jnp.stack([by_pair(queries), by_pair(key_proj), by_pair(value_proj), by_p...]
where the time goes in v2:
time: 105 us
  starting transfers between devices  30.4 us (29%)
  blocking collectives  29.1 us (28%)
  waiting for transfers between devices  26.3 us (25%)
  local copies, waits for them, and re-layouts  12 us (11%)
  matrix products  5.36 us (5%)
    psum x1, blocking collectives, local(): grad_gate = lax.psum(pair_terms, 'frame')  29.1 us
    all_to_all x1, waiting for transfers between devices, local(): lax.all_to_all(stacked, 'space', split_axis=0, concat_axis=2, tiled=True)  26.3 us
    all_to_all x1, starting transfers between devices, local(): lax.all_to_all(stacked, 'space', split_axis=0, concat_axis=2, tiled=True)  19.3 us
    all_to_all x1, starting transfers between devices, local(): lax.all_to_all(grads, 'space', split_axis=2, concat_axis=0, tiled=True)  11.1 us
    another operation x4, local copies, waits for them, and re-layouts, local(): jnp.stack([by_pair(queries), by_pair(key_proj), by_pair(value_proj), by_p...  4.22 us
    reshape x3, local copies, waits for them, and re-layouts, by_width(): return tensor.reshape(frames_local, pixels_local, clip_count, channels)  2.4 us
  transfers between devices with their start and end apart: 2, of which 1 were waited for; matrix products, arithmetic and copies ran while one was open for 0% of the time, Pallas kernels for 0%

profile of v2, /device:TPU:6, one launch (start us, length us, event | category | flops | bytes accessed | tf_op | source)
XLA Modules:
  0.0 104.8 jit_solution(11347054782889273948)
XLA Ops:
  0.6 0.0 copy-start
  0.6 1.1 %stack_reshape.12 = bf16[1,15,64,1,128]{4,2,1,3,0:T(8,128)(2,1)S(1)} reshape(bf16[1,15,8,1024]{3,2,1,0:T(8,128)(2,1)} %param.5) | data formatting | bytes 491520 | tf_op jit(solution)/shard_map/stack;reshape | solution.py:62
  1.7 1.1 %stack_reshape.13 = bf16[1,15,64,1,128]{4,2,1,3,0:T(8,128)(2,1)S(1)} reshape(bf16[1,15,8,1024]{3,2,1,0:T(8,128)(2,1)} %param.6) | data formatting | bytes 491520 | tf_op jit(solution)/shard_map/stack;reshape | solution.py:62
  2.8 1.1 %stack_reshape.14 = bf16[1,15,64,1,128]{4,2,1,3,0:T(8,128)(2,1)S(1)} reshape(bf16[1,15,8,1024]{3,2,1,0:T(8,128)(2,1)} %param.7) | data formatting | bytes 491520 | tf_op jit(solution)/shard_map/stack;reshape | solution.py:62
  3.8 1.1 %stack_reshape.15 = bf16[1,15,64,1,128]{4,2,1,3,0:T(8,128)(2,1)S(1)} reshape(bf16[1,15,8,1024]{3,2,1,0:T(8,128)(2,1)} %param.8) | data formatting | bytes 491520 | tf_op jit(solution)/shard_map/stack;reshape | solution.py:62
  4.9 0.1 maximum_bitcast_fusion
  5.0 1.7 %copy.35 = bf16[64,1,15,4,128]{4,3,2,1,0:T(4,128)(2,1)} copy(bf16[64,1,15,4,128]{4,0,2,3,1:T(8,128)(2,1)S(1)} %maximum_bitcast_fusion) | data formatting | bytes 1966080 | tf_op jit(solution)/shard_map/transpose | solution.py:63
  6.7 19.3 %all-to-all-start = ((bf16[64,1,15,4,128]{4,3,2,1,0:T(4,128)(2,1)}), bf16[64,1,15,4,128]{4,3,2,1,0:T(4,128)(2,1)S(1)}, u32[]{:S(2)}, u32[]{:S(2)}) async-start(bf16[64,1,15,4,128]{4,3,2,1,0:T(4,128)(2,1)} %copy.35), calls=%async_computation | async-start | bytes 1966080 | tf_op jit(solution)/shard_map/all_to_all | solution.py:64
  26.0 0.0 copy-done
  26.1 26.3 %all-to-all-done = bf16[64,1,15,4,128]{4,3,2,1,0:T(4,128)(2,1)S(1)} async-done(((bf16[64,1,15,4,128]{4,3,2,1,0:T(4,128)(2,1)}), bf16[64,1,15,4,128]{4,3,2,1,0:T(4,128)(2,1)S(1)}, u32[]{:S(2)}, u32[]{:S(2)}) %all-to-all-start) | async-done | bytes 983072 | tf_op jit(solution)/shard_map/all_to_all | solution.py:64
  52.3 1.4 %fusion.34 = (bf16[1,1,960,1,128]{4,3,2,1,0:T(2,128)(2,1)S(1)}, bf16[1,1,960,1,128]{4,3,2,1,0:T(2,128)(2,1)S(1)}, bf16[1,1,960,1,128]{4,3,2,1,0:T(2,128)(2,1)S(1)}, bf16[1,1,960,1,128]{4,3,2,1,0:T(2,128)(2,1)S(1)}) fusion(bf16[1,1,960,4,128]{4,3,2,1,0:T(4,128)(2,1)S(1)} %bitcast.91), kind=kLoop, calls=%fused_computation.45 | loop fusion | bytes 1966080 | tf_op jit(solution)/shard_map/slice | solution.py:66
  53.8 0.7 multiply_reduce_fusion
  54.5 0.7 fusion.1
  55.2 1.2 %fusion.13 = (f32[128]{0:T(128)S(1)}, f32[960]{0:T(1024)S(1)}, bf16[1,1,960,1,128]{4,2,3,1,0:T(8,128)(2,1)S(1)}) fusion(f32[128]{0:T(128)S(1)} %dynamic-slice_bitcast_fusion, bf16[1,1,960,1,128]{4,3,2,1,0:T(2,128)(2,1)S(1)} %get-tuple-element.7, bf16[1,1,960,1,128]{4,3,2,1,0:T(2,128)(2,1)S(1)} %get-tuple-element.8, f32[960]{0:T(1024)S(1)} %fusion.1, ...), kind=kOutput, calls=%fused_computation.23 | convolution fusion | flops 240597952 | bytes 4436224 | tf_op jit(solution)/shard_map/vmap(vmap())/dot_general | solution.py:27
  56.3 1.2 %multiply_convert_fusion = bf16[960,960]{0,1:T(8,128)(2,1)S(1)} fusion(f32[960]{0:T(1024)S(1)} %get-tuple-element.5, bf16[1,1,960,1,128]{4,2,3,1,0:T(8,128)(2,1)S(1)} %get-tuple-element.6, f32[128]{0:T(128)S(1)} %dynamic-slice_bitcast_fusion, bf16[1,1,960,1,128]{4,3,2,1,0:T(2,128)(2,1)S(1)} %get-tuple-element.8, f32[960]{0:T(1024)S(1)} %fusion.1, ...), kind=kOutput, calls=%fused_computation | convolution fusion | flops 241827840 | bytes 6033152 | tf_op jit(solution)/shard_map/vmap(vmap())/dot_general | solution.py:31
  57.5 0.8 fusion.5
  58.3 0.7 fusion.4
  59.0 0.9 fusion.6
  59.9 0.1 pad_maximum_fusion
  60.0 0.6 copy.38
  60.6 1.3 %reshape_transpose.3 = bf16[1,1,64,45,128]{4,3,2,1,0:T(8,128)(2,1)} reshape(bf16[1,960,1,3,128]{4,3,1,2,0:T(4,128)(2,1)S(1)} %copy.38) | data formatting | bytes 1474560 | tf_op jit(solution)/shard_map/reshape;transpose | solution.py:78
  61.9 11.1 %all-to-all-start.1 = ((bf16[1,1,64,45,128]{4,3,1,0,2:T(8,128)(2,1)}), bf16[1,1,64,45,128]{4,3,1,0,2:T(8,128)(2,1)S(1)}, u32[]{:S(2)}, u32[]{:S(2)}) async-start(bf16[1,1,64,45,128]{4,3,1,0,2:T(8,128)(2,1)} %bitcast.12), calls=%async_computation.1 | async-start | bytes 1572864 | tf_op jit(solution)/shard_map/all_to_all | solution.py:79
  73.1 29.1 %psum.7 = f32[1,128]{1,0:T(1,128)} all-reduce(f32[1,128]{1,0:T(1,128)S(1)} %bitcast.93), channel_id=1, replica_groups=mesh['frame'=8,'space'=64] {'frame'}, use_global_device_ids=true, to_apply=%region_4.0 | all-reduce | flops 128 | bytes 1024 | tf_op jit(solution)/shard_map/psum | solution.py:85
  102.2 0.0 all-to-all-done.1
  102.2 0.2 copy.40
  102.4 0.1 slice_bitcast_fusion
  102.4 0.8 reshape.150
  103.2 0.8 reshape.151
  104.0 0.8 reshape.152
  (2 shorter events, 0.0 us)
Async XLA Ops:
  0.6 25.4 %copy-start = (f32[8,1024]{1,0:T(8,128)S(1)}, f32[8,1024]{1,0:T(8,128)}, u32[]{:S(2)}) copy-start(f32[8,1024]{1,0:T(8,128)} %param.9) | copy-start | bytes 98308
  6.7 45.6 %all-to-all-start = ((bf16[64,1,15,4,128]{4,3,2,1,0:T(4,128)(2,1)}), bf16[64,1,15,4,128]{4,3,2,1,0:T(4,128)(2,1)S(1)}, u32[]{:S(2)}, u32[]{:S(2)}) async-start(bf16[64,1,15,4,128]{4,3,2,1,0:T(4,128)(2,1)} %copy.35), calls=%async_computation | async-start | bytes 1966080 | tf_op jit(solution)/shard_map/all_to_all | solution.py:64
  61.9 40.2 %all-to-all-start.1 = ((bf16[1,1,64,45,128]{4,3,1,0,2:T(8,128)(2,1)}), bf16[1,1,64,45,128]{4,3,1,0,2:T(8,128)(2,1)S(1)}, u32[]{:S(2)}, u32[]{:S(2)}) async-start(bf16[1,1,64,45,128]{4,3,1,0,2:T(8,128)(2,1)} %bitcast.12), calls=%async_computation.1 | async-start | bytes 1572864 | tf_op jit(solution)/shard_map/all_to_all | solution.py:79

commit v3 on v2

--- a/solution.py
+++ b/solution.py
@@ -3,6 +3,7 @@
 import jax
 import jax.numpy as jnp
 from jax import lax
+from jax.experimental import pallas as pl
 from jax.sharding import PartitionSpec as P
 
 DH = 128
@@ -46,6 +47,50 @@
     return (grad_query, grad_key, grad_value, attended, gate_part)
 
 
+def attention_kernel(q_ref, k_ref, v_ref, up_ref, gate_ref, gq_ref, gk_ref, gv_ref, gp_ref):
+    query_one = q_ref[...]
+    key_one = k_ref[...]
+    value_one = v_ref[...]
+    inv_root = 1.0 / math.sqrt(query_one.shape[1])
+    by_last = (((1,), (1,)), ((), ()))
+    by_first = (((0,), (0,)), ((), ()))
+    scores = lax.dot_general(query_one, key_one, by_last, preferred_element_type=jnp.float32) * inv_root
+    row_peak = jnp.max(scores, axis=-1, keepdims=True)
+    exp_terms = jnp.exp(scores - row_peak)
+    attention = exp_terms / jnp.sum(exp_terms, axis=-1, keepdims=True)
+    attention_low = attention.astype(jnp.bfloat16)
+    attended = jnp.dot(attention_low, value_one, preferred_element_type=jnp.float32)
+    upstream_wide = up_ref[...].astype(jnp.float32)
+    cotangent = (gate_ref[...] * upstream_wide).astype(jnp.bfloat16)
+    gp_ref[...] = jnp.sum(upstream_wide * attended, axis=0, keepdims=True)
+    grad_attn = lax.dot_general(cotangent, value_one, by_last, preferred_element_type=jnp.float32)
+    row_terms = jnp.sum(cotangent.astype(jnp.float32) * attended, axis=-1, keepdims=True)
+    grad_scores = (attention * (grad_attn - row_terms)).astype(jnp.bfloat16)
+    gq_ref[...] = (jnp.dot(grad_scores, key_one, preferred_element_type=jnp.float32) * inv_root).astype(
+        jnp.bfloat16
+    )
+    gk_ref[...] = (
+        lax.dot_general(grad_scores, query_one, by_first, preferred_element_type=jnp.float32) * inv_root
+    ).astype(jnp.bfloat16)
+    gv_ref[...] = lax.dot_general(
+        attention_low, cotangent, by_first, preferred_element_type=jnp.float32
+    ).astype(jnp.bfloat16)
+
+
+def attention_grads(query_all, key_all, value_all, upstream_all, gate_all):
+    items, rows, channels = query_all.shape
+    row_block = pl.BlockSpec((None, rows, channels), lambda i: (i, 0, 0))
+    gate_block = pl.BlockSpec((None, 1, channels), lambda i: (i, 0, 0))
+    grad_shape = jax.ShapeDtypeStruct((items, rows, channels), jnp.bfloat16)
+    return pl.pallas_call(
+        attention_kernel,
+        grid=(items,),
+        in_specs=[row_block, row_block, row_block, row_block, gate_block],
+        out_specs=[row_block, row_block, row_block, gate_block],
+        out_shape=[grad_shape, grad_shape, grad_shape, jax.ShapeDtypeStruct((items, 1, channels), jnp.float32)],
+    )(query_all, key_all, value_all, upstream_all, gate_all)
+
+
 def local(queries, key_proj, value_proj, grad_out, gate_vec):
     frames_local, pixels_local, clip_count, channels = queries.shape
     head_count = channels // DH
@@ -62,26 +107,25 @@
     stacked = jnp.stack([by_pair(queries), by_pair(key_proj), by_pair(value_proj), by_pair(grad_out)], axis=3)
     stacked = jnp.transpose(stacked, (2, 0, 1, 3, 4))
     gathered = lax.all_to_all(stacked, "space", split_axis=0, concat_axis=2, tiled=True)
+    items = pairs_local * frames_local
     query_all, key_all, value_all, upstream_all = (
-        jnp.transpose(gathered[:, :, :, part, :], (1, 2, 0, 3)) for part in range(4)
+        gathered[:, :, :, part, :].reshape(items, -1, DH) for part in range(4)
     )
     gate_rows = lax.dynamic_slice_in_dim(
         gate_vec.reshape(pair_count, DH), lax.axis_index("space") * pairs_local, pairs_local, 0
     )
-    per_pair = jax.vmap(item_grads, in_axes=(1, 1, 1, 1, 0), out_axes=(1, 1, 1, 1, 0))
-    per_frame = jax.vmap(per_pair, in_axes=(0, 0, 0, 0, None), out_axes=0)
-    grad_query, grad_key, grad_value, attended, gate_parts = per_frame(
-        query_all, key_all, value_all, upstream_all, gate_rows
+    gate_all = jnp.broadcast_to(gate_rows[:, None, None, :], (pairs_local, frames_local, 1, DH))
+    grad_query, grad_key, grad_value, gate_parts = attention_grads(
+        query_all, key_all, value_all, upstream_all, gate_all.reshape(items, 1, DH)
     )
-    grads = jnp.stack([grad_query, grad_key, grad_value], axis=3)
-    grads = jnp.transpose(grads, (2, 0, 1, 3, 4))
+    grads = jnp.stack([grad_query, grad_key, grad_value], axis=2)
     grads = grads.reshape(pairs_local, frames_local, space_size, pixels_local * 3, DH)
     back = lax.all_to_all(grads, "space", split_axis=2, concat_axis=0, tiled=True)
     back = back.reshape(pair_count, frames_local, pixels_local, 3, DH)
     back_query, back_key, back_value = (
         jnp.transpose(back[:, :, :, part, :], (1, 2, 0, 3)) for part in range(3)
     )
-    pair_terms = jnp.sum(gate_parts, axis=0)
+    pair_terms = jnp.sum(gate_parts.reshape(pairs_local, frames_local, DH), axis=1)
     grad_gate = lax.psum(pair_terms, "frame")
     return (by_width(back_query), by_width(back_key), by_width(back_value), grad_gate)
 

time: 105 us -> 108 us (1.029)
  Pallas kernels: 0 us -> 7.07 us
  matrix products: 5.36 us -> 0 us
  local copies, waits for them, and re-layouts: 12 us -> 13.7 us
    pallas_call x0 -> x1, Pallas kernels: none -> 7.07 us  [attention_grads(): pl.pallas_call(attention_kernel, grid=(items,), in_specs=[row_block, row_...]
    dot_general x6 -> x0, matrix products: 5.36 us -> none  [the longest x1 1.16 us: item_grads(): jnp.dot(attention_low, value_one, preferred_element_type=jnp.float32)]
    another operation x4, local copies, waits for them, and re-layouts: 4.22 us -> 1.42 us  [local(): jnp.stack([by_pair(queries), by_pair(key_proj), by_pair(value_proj), by_p...]
    unnamed x2 -> x10, local copies, waits for them, and re-layouts: 0.01 us -> 2.32 us
    reshape x0 -> x1, local copies, waits for them, and re-layouts: none -> 1.34 us  [local(): grads.reshape(pairs_local, frames_local, space_size, pixels_local * 3, DH)]
    another operation x1, other arithmetic: 0.08 us -> 1.26 us  [local(): grads = jnp.stack([grad_query, grad_key, grad_value], axis=2)]
    another operation x2 -> x4, local copies, waits for them, and re-layouts: 1.98 us -> 2.85 us  [the longest x2 1.69 us: local(): gathered[:, :, :, part, :].reshape(items, -1, DH)]
where the time goes in v3:
time: 108 us
  starting transfers between devices  30.5 us (28%)
  blocking collectives  28.4 us (26%)
  waiting for transfers between devices  25.8 us (24%)
  local copies, waits for them, and re-layouts  13.7 us (13%)
  Pallas kernels  7.07 us (7%)
  other arithmetic  1.39 us (1%)
    psum x1, blocking collectives, local(): grad_gate = lax.psum(pair_terms, 'frame')  28.4 us
    all_to_all x1, waiting for transfers between devices, local(): lax.all_to_all(stacked, 'space', split_axis=0, concat_axis=2, tiled=True)  25.8 us
    all_to_all x1, starting transfers between devices, local(): lax.all_to_all(stacked, 'space', split_axis=0, concat_axis=2, tiled=True)  19.4 us
    all_to_all x1, starting transfers between devices, local(): lax.all_to_all(grads, 'space', split_axis=2, concat_axis=0, tiled=True)  11.1 us
    pallas_call x1, Pallas kernels, attention_grads(): pl.pallas_call(attention_kernel, grid=(items,), in_specs=[row_block, row_...  7.07 us
    reshape x3, local copies, waits for them, and re-layouts, by_width(): return tensor.reshape(frames_local, pixels_local, clip_count, channels)  2.4 us
    unnamed x10, local copies, waits for them, and re-layouts  2.32 us
  transfers between devices with their start and end apart: 2, of which 1 were waited for; matrix products, arithmetic and copies ran while one was open for 0% of the time, Pallas kernels for 0%

profile of v3, /device:TPU:6, one launch (start us, length us, event | category | flops | bytes accessed | tf_op | source)
XLA Modules:
  0.0 107.7 jit_solution(2527119100239814285)
XLA Ops:
  0.6 0.0 copy-start
  0.6 1.1 %stack_reshape.12 = bf16[1,15,64,1,128]{4,2,1,3,0:T(8,128)(2,1)S(1)} reshape(bf16[1,15,8,1024]{3,2,1,0:T(8,128)(2,1)} %param.5) | data formatting | bytes 491520 | tf_op jit(solution)/shard_map/stack;reshape | solution.py:107
  1.7 0.0 copy-done
  1.7 0.0 copy-start.1
  1.8 0.1 stack_reshape.13
  1.9 0.8 copy-done.1
  2.7 0.0 copy-start.2
  2.7 0.1 stack_reshape.14
  2.8 0.8 copy-done.2
  3.6 0.1 stack_reshape.15
  3.8 0.1 maximum_bitcast_fusion
  3.9 1.7 %copy.30 = bf16[64,1,15,4,128]{4,3,2,1,0:T(4,128)(2,1)} copy(bf16[64,1,15,4,128]{4,0,2,3,1:T(8,128)(2,1)S(1)} %maximum_bitcast_fusion) | data formatting | bytes 1966080 | tf_op jit(solution)/shard_map/transpose | solution.py:108
  5.6 0.0 copy-start.3
  5.6 19.4 %all-to-all-start = ((bf16[64,1,15,4,128]{4,3,2,1,0:T(4,128)(2,1)}), bf16[64,1,15,4,128]{4,3,2,1,0:T(4,128)(2,1)S(1)}, u32[]{:S(2)}, u32[]{:S(2)}) async-start(bf16[64,1,15,4,128]{4,3,2,1,0:T(4,128)(2,1)} %copy.30), calls=%async_computation | async-start | bytes 1966080 | tf_op jit(solution)/shard_map/all_to_all | solution.py:109
  25.0 0.0 copy-done.3
  25.0 0.5 dynamic-slice_bitcast_fusion.gate_ref
  25.6 25.8 %all-to-all-done = bf16[64,1,15,4,128]{4,3,2,1,0:T(4,128)(2,1)S(1)} async-done(((bf16[64,1,15,4,128]{4,3,2,1,0:T(4,128)(2,1)}), bf16[64,1,15,4,128]{4,3,2,1,0:T(4,128)(2,1)S(1)}, u32[]{:S(2)}, u32[]{:S(2)}) %all-to-all-start) | async-done | bytes 983072 | tf_op jit(solution)/shard_map/all_to_all | solution.py:109
  51.3 1.4 %fusion = (bf16[1,1,960,1,128]{4,3,2,1,0:T(2,128)(2,1)S(1)}, bf16[1,1,960,1,128]{4,3,2,1,0:T(2,128)(2,1)S(1)}, bf16[1,1,960,1,128]{4,3,2,1,0:T(2,128)(2,1)S(1)}, bf16[1,1,960,1,128]{4,3,2,1,0:T(2,128)(2,1)S(1)}) fusion(bf16[1,1,960,4,128]{4,3,2,1,0:T(4,128)(2,1)S(1)} %bitcast.45), kind=kLoop, calls=%fused_computation.10 | loop fusion | bytes 1966080 | tf_op jit(solution)/shard_map/slice | solution.py:112
  52.8 0.9 copy_bitcast_fusion
  53.6 0.8 copy_bitcast_fusion.2
  54.5 7.1 %shard_map.84 = (bf16[1,960,128]{2,1,0:T(8,128)(2,1)}, bf16[1,960,128]{2,1,0:T(8,128)(2,1)}, bf16[1,960,128]{2,1,0:T(8,128)(2,1)}, f32[1,1,128]{2,1,0:T(1,128)}) custom-call(bf16[1,960,128]{2,1,0:T(8,128)(2,1)} %get-tuple-element.22.q_ref, bf16[1,960,128]{2,1,0:T(8,128)(2,1)} %get-tuple-element.21.k_ref, bf16[1,960,128]{2,1,0:T(8,128)(2,1)} %get-tuple-element.20.v_ref, ...), custom_call_target="tpu_custom_call" | custom-call | tf_op jit(solution)/shard_map/pallas_call | solution.py:85
  61.6 1.3 %pad_maximum_fusion = bf16[1,960,3,128]{3,1,2,0:T(8,128)(2,1)S(1)} fusion(bf16[1,960,1,128]{3,1,2,0:T(8,128)(2,1)} %bitcast.49, bf16[1,960,1,128]{3,1,2,0:T(8,128)(2,1)} %bitcast.48, bf16[1,960,1,128]{3,1,2,0:T(8,128)(2,1)} %bitcast.47), kind=kLoop, calls=%fused_computation.1 | loop fusion | flops 737280 | bytes 1474560 | tf_op jit(solution)/shard_map/stack | solution.py:121
  62.8 0.6 copy.35
  63.5 1.3 %reshape.35 = bf16[1,1,64,45,128]{4,3,2,1,0:T(8,128)(2,1)} reshape(bf16[1,960,3,128]{3,2,1,0:T(4,128)(2,1)S(1)} %copy.35) | data formatting | bytes 1474560 | tf_op jit(solution)/shard_map/reshape | solution.py:122
  64.8 11.1 %all-to-all-start.1 = ((bf16[1,1,64,45,128]{4,3,1,0,2:T(8,128)(2,1)}), bf16[1,1,64,45,128]{4,3,1,0,2:T(8,128)(2,1)S(1)}, u32[]{:S(2)}, u32[]{:S(2)}) async-start(bf16[1,1,64,45,128]{4,3,1,0,2:T(8,128)(2,1)} %bitcast.10), calls=%async_computation.1 | async-start | bytes 1572864 | tf_op jit(solution)/shard_map/all_to_all | solution.py:123
  75.9 0.0 copy-start.4
  76.0 0.7 copy-done.4
  76.6 28.4 %psum.7 = f32[1,128]{1,0:T(1,128)} all-reduce(f32[1,128]{1,0:T(1,128)S(1)} %bitcast.50), channel_id=1, replica_groups=mesh['frame'=8,'space'=64] {'frame'}, use_global_device_ids=true, to_apply=%region_0.0 | all-reduce | flops 128 | bytes 1024 | tf_op jit(solution)/shard_map/psum | solution.py:129
  105.0 0.0 all-to-all-done.1
  105.0 0.2 copy.37
  105.2 0.1 slice_bitcast_fusion
  105.3 0.8 reshape.37
  106.1 0.8 reshape.38
  106.9 0.8 reshape.39
  (1 shorter events, 0.0 us)
Async XLA Ops:
  0.6 1.1 %copy-start = (bf16[1,15,8,1024]{3,2,1,0:T(8,128)(2,1)S(1)}, bf16[1,15,8,1024]{3,2,1,0:T(8,128)(2,1)}, u32[]{:S(2)}) copy-start(bf16[1,15,8,1024]{3,2,1,0:T(8,128)(2,1)} %param.6) | copy-start | bytes 737284
  1.7 0.9 copy-start.1
  2.7 0.9 copy-start.2
  5.6 19.4 %copy-start.3 = (f32[8,1024]{1,0:T(8,128)S(1)}, f32[8,1024]{1,0:T(8,128)}, u32[]{:S(2)}) copy-start(f32[8,1024]{1,0:T(8,128)} %param.9) | copy-start | bytes 98308
  5.6 45.8 %all-to-all-start = ((bf16[64,1,15,4,128]{4,3,2,1,0:T(4,128)(2,1)}), bf16[64,1,15,4,128]{4,3,2,1,0:T(4,128)(2,1)S(1)}, u32[]{:S(2)}, u32[]{:S(2)}) async-start(bf16[64,1,15,4,128]{4,3,2,1,0:T(4,128)(2,1)} %copy.30), calls=%async_computation | async-start | bytes 1966080 | tf_op jit(solution)/shard_map/all_to_all | solution.py:109
  64.8 40.2 %all-to-all-start.1 = ((bf16[1,1,64,45,128]{4,3,1,0,2:T(8,128)(2,1)}), bf16[1,1,64,45,128]{4,3,1,0,2:T(8,128)(2,1)S(1)}, u32[]{:S(2)}, u32[]{:S(2)}) async-start(bf16[1,1,64,45,128]{4,3,1,0,2:T(8,128)(2,1)} %bitcast.10), calls=%async_computation.1 | async-start | bytes 1572864 | tf_op jit(solution)/shard_map/all_to_all | solution.py:123
  75.9 0.7 copy-start.4

commit v4 on v2

--- a/solution.py
+++ b/solution.py
@@ -59,11 +59,13 @@
 
     space_size = lax.axis_size("space")
     pairs_local = pair_count // space_size
-    stacked = jnp.stack([by_pair(queries), by_pair(key_proj), by_pair(value_proj), by_pair(grad_out)], axis=3)
-    stacked = jnp.transpose(stacked, (2, 0, 1, 3, 4))
+    stacked = jnp.concatenate(
+        [by_pair(t) for t in (queries, key_proj, value_proj, grad_out)], axis=3
+    )
+    stacked = jnp.transpose(stacked, (2, 0, 1, 3))
     gathered = lax.all_to_all(stacked, "space", split_axis=0, concat_axis=2, tiled=True)
     query_all, key_all, value_all, upstream_all = (
-        jnp.transpose(gathered[:, :, :, part, :], (1, 2, 0, 3)) for part in range(4)
+        jnp.transpose(gathered[:, :, :, part * DH:(part + 1) * DH], (1, 2, 0, 3)) for part in range(4)
     )
     gate_rows = lax.dynamic_slice_in_dim(
         gate_vec.reshape(pair_count, DH), lax.axis_index("space") * pairs_local, pairs_local, 0
@@ -73,13 +75,12 @@
     grad_query, grad_key, grad_value, attended, gate_parts = per_frame(
         query_all, key_all, value_all, upstream_all, gate_rows
     )
-    grads = jnp.stack([grad_query, grad_key, grad_value], axis=3)
-    grads = jnp.transpose(grads, (2, 0, 1, 3, 4))
-    grads = grads.reshape(pairs_local, frames_local, space_size, pixels_local * 3, DH)
+    grads = jnp.stack([grad_query, grad_key, grad_value], axis=0)
+    grads = grads.reshape(3, frames_local, space_size, pixels_local, pairs_local, DH)
+    grads = jnp.transpose(grads, (4, 1, 2, 0, 3, 5))
     back = lax.all_to_all(grads, "space", split_axis=2, concat_axis=0, tiled=True)
-    back = back.reshape(pair_count, frames_local, pixels_local, 3, DH)
     back_query, back_key, back_value = (
-        jnp.transpose(back[:, :, :, part, :], (1, 2, 0, 3)) for part in range(3)
+        jnp.transpose(back[:, :, 0, part], (1, 2, 0, 3)) for part in range(3)
     )
     pair_terms = jnp.sum(gate_parts, axis=0)
     grad_gate = lax.psum(pair_terms, "frame")

time: 105 us -> 105 us (level)
  local copies, waits for them, and re-layouts: 12 us -> 10.1 us
    another operation x6 -> x3, local copies, waits for them, and re-layouts: 6.2 us -> 0.26 us  [local(): grads = jnp.stack([grad_query, grad_key, grad_value], axis=0)]
    reshape x0 -> x4, local copies, waits for them, and re-layouts: none -> 4.22 us  [by_pair(): return tensor.reshape(frames_local, pixels_local, pair_count, DH)]
    slice x1 -> x0, local copies, waits for them, and re-layouts: 1.43 us -> none  [local(): gathered[:, :, :, part, :]]
    transpose x2 -> x6, local copies, waits for them, and re-layouts: 1.76 us -> 2.88 us  [the longest x1 1.53 us: local(): stacked = jnp.transpose(stacked, (2, 0, 1, 3))]
where the time goes in v4:
time: 105 us; the launch traced here: 104 us
  starting transfers between devices  31 us (30%)
  blocking collectives  29.1 us (28%)
  waiting for transfers between devices  27.1 us (26%)
  local copies, waits for them, and re-layouts  10.1 us (10%)
  matrix products  5.31 us (5%)
    psum x1, blocking collectives, local(): grad_gate = lax.psum(pair_terms, 'frame')  29.1 us
    all_to_all x1, waiting for transfers between devices, local(): lax.all_to_all(stacked, 'space', split_axis=0, concat_axis=2, tiled=True)  27.1 us
    all_to_all x1, starting transfers between devices, local(): lax.all_to_all(stacked, 'space', split_axis=0, concat_axis=2, tiled=True)  19.3 us
    all_to_all x1, starting transfers between devices, local(): lax.all_to_all(grads, 'space', split_axis=2, concat_axis=0, tiled=True)  11.7 us
    reshape x4, local copies, waits for them, and re-layouts, by_pair(): return tensor.reshape(frames_local, pixels_local, pair_count, DH)  4.22 us
    reshape x3, local copies, waits for them, and re-layouts, by_width(): return tensor.reshape(frames_local, pixels_local, clip_count, channels)  2.4 us
  transfers between devices with their start and end apart: 2, of which 1 were waited for; matrix products, arithmetic and copies ran while one was open for 0% of the time, Pallas kernels for 0%

profile of v4, /device:TPU:6, one launch (start us, length us, event | category | flops | bytes accessed | tf_op | source)
XLA Modules:
  0.0 104.4 jit_solution(6389578511602308686)
XLA Ops:
  0.6 0.0 copy-start
  0.6 1.1 %reshape.140 = bf16[1,15,64,128]{3,2,1,0:T(8,128)(2,1)S(1)} reshape(bf16[1,15,8,1024]{3,2,1,0:T(8,128)(2,1)} %param.5) | data formatting | bytes 491520 | tf_op jit(solution)/shard_map/reshape | solution.py:55
  1.7 1.1 %reshape.141 = bf16[1,15,64,128]{3,2,1,0:T(8,128)(2,1)S(1)} reshape(bf16[1,15,8,1024]{3,2,1,0:T(8,128)(2,1)} %param.6) | data formatting | bytes 491520 | tf_op jit(solution)/shard_map/reshape | solution.py:55
  2.8 1.1 %reshape.142 = bf16[1,15,64,128]{3,2,1,0:T(8,128)(2,1)S(1)} reshape(bf16[1,15,8,1024]{3,2,1,0:T(8,128)(2,1)} %param.7) | data formatting | bytes 491520 | tf_op jit(solution)/shard_map/reshape | solution.py:55
  3.8 1.1 %reshape.143 = bf16[1,15,64,128]{3,2,1,0:T(8,128)(2,1)S(1)} reshape(bf16[1,15,8,1024]{3,2,1,0:T(8,128)(2,1)} %param.8) | data formatting | bytes 491520 | tf_op jit(solution)/shard_map/reshape | solution.py:55
  4.9 0.1 maximum_bitcast_fusion
  5.0 1.5 %copy.35 = bf16[64,1,15,512]{3,2,1,0:T(8,128)(2,1)} copy(bf16[64,1,15,512]{3,0,2,1:T(8,128)(2,1)S(1)} %maximum_bitcast_fusion) | data formatting | bytes 1966080 | tf_op jit(solution)/shard_map/transpose | solution.py:65
  6.5 19.3 %all-to-all-start = ((bf16[64,1,15,512]{3,2,1,0:T(8,128)(2,1)}), bf16[64,1,15,512]{3,2,1,0:T(8,128)(2,1)S(1)}, u32[]{:S(2)}, u32[]{:S(2)}) async-start(bf16[64,1,15,512]{3,2,1,0:T(8,128)(2,1)} %copy.35), calls=%async_computation | async-start | bytes 2097152 | tf_op jit(solution)/shard_map/all_to_all | solution.py:66
  25.8 0.0 copy-done
  25.9 27.1 %all-to-all-done = bf16[64,1,15,512]{3,2,1,0:T(8,128)(2,1)S(1)} async-done(((bf16[64,1,15,512]{3,2,1,0:T(8,128)(2,1)}), bf16[64,1,15,512]{3,2,1,0:T(8,128)(2,1)S(1)}, u32[]{:S(2)}, u32[]{:S(2)}) %all-to-all-start) | async-done | bytes 983072 | tf_op jit(solution)/shard_map/all_to_all | solution.py:66
  53.0 0.3 all_to_all.9
  53.3 0.7 multiply_reduce_fusion
  54.0 0.7 fusion.1
  54.7 1.1 %fusion.10 = (f32[128]{0:T(128)S(1)}, f32[960]{0:T(1024)S(1)}) fusion(bf16[1,1,960,512]{3,2,1,0:T(8,128)(2,1)S(1)} %all_to_all.9, f32[128]{0:T(128)S(1)} %dynamic-slice_bitcast_fusion, f32[960]{0:T(1024)S(1)} %fusion.1, f32[960]{0:T(1024)S(1)} %get-tuple-element.9, f32[960,960]{0,1:T(8,128)S(1)} %get-tuple-element.10), kind=kOutput, calls=%fused_computation.20 | convolution fusion | flops 240597952 | bytes 4436736 | tf_op jit(solution)/shard_map/vmap(vmap())/dot_general | solution.py:27
  55.8 0.9 convolution_convert_fusion
  56.7 1.1 %multiply_convert_fusion = bf16[960,960]{0,1:T(8,128)(2,1)S(1)} fusion(f32[960]{0:T(1024)S(1)} %get-tuple-element.5, bf16[1,1,960,512]{3,2,1,0:T(8,128)(2,1)S(1)} %all_to_all.9, f32[128]{0:T(128)S(1)} %dynamic-slice_bitcast_fusion, f32[960]{0:T(1024)S(1)} %fusion.1, f32[960]{0:T(1024)S(1)} %get-tuple-element.9, f32[960,960]{0,1:T(8,128)S(1)} %get-tuple-element.10), kind=kOutput, calls=%fused_computation | convolution fusion | flops 241827840 | bytes 6279680 | tf_op jit(solution)/shard_map/vmap(vmap())/dot_general | solution.py:31
  57.9 0.7 fusion.3
  58.5 0.8 fusion.2
  59.3 0.1 stack.11
  59.4 0.1 stack.9
  59.5 0.1 stack.10
  59.6 0.2 maximum_bitcast_fusion.1
  59.8 1.0 copy.37
  60.8 11.7 %all-to-all-start.1 = ((bf16[1,1,64,3,15,128]{5,4,0,1,3,2:T(8,128)(2,1)}), bf16[1,1,64,3,15,128]{5,4,0,1,3,2:T(8,128)(2,1)S(1)}, u32[]{:S(2)}, u32[]{:S(2)}) async-start(bf16[1,1,64,3,15,128]{5,4,0,1,3,2:T(8,128)(2,1)} %copy.37), calls=%async_computation.1 | async-start | bytes 1572864 | tf_op jit(solution)/shard_map/all_to_all | solution.py:81
  72.5 29.1 %psum.7 = f32[1,128]{1,0:T(1,128)} all-reduce(f32[1,128]{1,0:T(1,128)S(1)} %bitcast.79), channel_id=1, replica_groups=mesh['frame'=8,'space'=64] {'frame'}, use_global_device_ids=true, to_apply=%region_4.0 | all-reduce | flops 128 | bytes 1024 | tf_op jit(solution)/shard_map/psum | solution.py:86
  101.6 0.0 all-to-all-done.1
  101.6 0.1 slice_bitcast_fusion
  101.8 0.1 copy.40
  101.9 0.8 reshape.153
  102.7 0.1 copy.39
  102.7 0.8 reshape.152
  103.5 0.1 copy.38
  103.6 0.8 reshape.151
  (2 shorter events, 0.0 us)
Async XLA Ops:
  0.6 25.2 %copy-start = (f32[8,1024]{1,0:T(8,128)S(1)}, f32[8,1024]{1,0:T(8,128)}, u32[]{:S(2)}) copy-start(f32[8,1024]{1,0:T(8,128)} %param.9) | copy-start | bytes 98308
  6.5 46.4 %all-to-all-start = ((bf16[64,1,15,512]{3,2,1,0:T(8,128)(2,1)}), bf16[64,1,15,512]{3,2,1,0:T(8,128)(2,1)S(1)}, u32[]{:S(2)}, u32[]{:S(2)}) async-start(bf16[64,1,15,512]{3,2,1,0:T(8,128)(2,1)} %copy.35), calls=%async_computation | async-start | bytes 2097152 | tf_op jit(solution)/shard_map/all_to_all | solution.py:66
  60.8 40.8 %all-to-all-start.1 = ((bf16[1,1,64,3,15,128]{5,4,0,1,3,2:T(8,128)(2,1)}), bf16[1,1,64,3,15,128]{5,4,0,1,3,2:T(8,128)(2,1)S(1)}, u32[]{:S(2)}, u32[]{:S(2)}) async-start(bf16[1,1,64,3,15,128]{5,4,0,1,3,2:T(8,128)(2,1)} %copy.37), calls=%async_computation.1 | async-start | bytes 1572864 | tf_op jit(solution)/shard_map/all_to_all | solution.py:81

commit v5 on v4

--- a/solution.py
+++ b/solution.py
@@ -59,10 +59,11 @@
 
     space_size = lax.axis_size("space")
     pairs_local = pair_count // space_size
-    stacked = jnp.concatenate(
-        [by_pair(t) for t in (queries, key_proj, value_proj, grad_out)], axis=3
-    )
-    stacked = jnp.transpose(stacked, (2, 0, 1, 3))
+    joined = jnp.concatenate([queries, key_proj, value_proj, grad_out], axis=3)
+    joined = joined.reshape(frames_local, pixels_local, clip_count, 4, head_count, DH)
+    picker = jnp.eye(clip_count, dtype=joined.dtype)
+    stacked = jnp.einsum("fibahd,bc->chfiad", joined, picker, preferred_element_type=jnp.float32)
+    stacked = stacked.astype(joined.dtype).reshape(pair_count, frames_local, pixels_local, 4 * DH)
     gathered = lax.all_to_all(stacked, "space", split_axis=0, concat_axis=2, tiled=True)
     query_all, key_all, value_all, upstream_all = (
         jnp.transpose(gathered[:, :, :, part * DH:(part + 1) * DH], (1, 2, 0, 3)) for part in range(4)

time: 105 us -> 103 us (0.981)
  local copies, waits for them, and re-layouts: 10.1 us -> 6.48 us
  other arithmetic: 1 us -> 2.25 us
    reshape x4 -> x2, local copies, waits for them, and re-layouts: 4.22 us -> 2.13 us  [local(): stacked.astype(joined.dtype)]
    transpose x1 -> x0, local copies, waits for them, and re-layouts: 1.53 us -> none  [local(): stacked = jnp.transpose(stacked, (2, 0, 1, 3))]
    concatenate x0 -> x1, other arithmetic: none -> 1.38 us  [local(): joined = jnp.concatenate([queries, key_proj, value_proj, grad_out], axis=3)]
where the time goes in v5:
time: 103 us; the launch traced here: 102 us
  starting transfers between devices  31 us (30%)
  blocking collectives  29.1 us (28%)
  waiting for transfers between devices  27.1 us (26%)
  local copies, waits for them, and re-layouts  6.48 us (6%)
  matrix products  5.71 us (6%)
  other arithmetic  2.25 us (2%)
    psum x1, blocking collectives, local(): grad_gate = lax.psum(pair_terms, 'frame')  29.1 us
    all_to_all x1, waiting for transfers between devices, local(): lax.all_to_all(stacked, 'space', split_axis=0, concat_axis=2, tiled=True)  27.1 us
    all_to_all x1, starting transfers between devices, local(): lax.all_to_all(stacked, 'space', split_axis=0, concat_axis=2, tiled=True)  19.3 us
    all_to_all x1, starting transfers between devices, local(): lax.all_to_all(grads, 'space', split_axis=2, concat_axis=0, tiled=True)  11.7 us
    reshape x3, local copies, waits for them, and re-layouts, by_width(): return tensor.reshape(frames_local, pixels_local, clip_count, channels)  2.4 us
    reshape x2, local copies, waits for them, and re-layouts, local(): stacked.astype(joined.dtype)  2.13 us
  transfers between devices with their start and end apart: 2, of which 1 were waited for; matrix products, arithmetic and copies ran while one was open for 0% of the time, Pallas kernels for 0%

profile of v5, /device:TPU:6, one launch (start us, length us, event | category | flops | bytes accessed | tf_op | source)
XLA Modules:
  0.0 102.4 jit_solution(2635578691211308121)
XLA Ops:
  0.6 1.4 %pad_maximum_fusion = bf16[1,15,8,4096]{3,2,1,0:T(8,128)(2,1)S(1)} fusion(bf16[1,15,8,1024]{3,2,1,0:T(8,128)(2,1)} %param.8, bf16[1,15,8,1024]{3,2,1,0:T(8,128)(2,1)} %param.7, bf16[1,15,8,1024]{3,2,1,0:T(8,128)(2,1)} %param.6, bf16[1,15,8,1024]{3,2,1,0:T(8,128)(2,1)} %param.5), kind=kLoop, calls=%fused_computation.12 | loop fusion | flops 3932160 | bytes 1966080 | tf_op jit(solution)/shard_map/concatenate | solution.py:62
  2.0 0.0 copy-start
  2.0 0.4 fusion.2
  2.4 0.8 copy.31
  3.2 1.4 %reshape.152 = bf16[64,1,15,512]{3,2,1,0:T(8,128)(2,1)} reshape(bf16[8,8,1,15,4,128]{5,4,3,1,0,2:T(4,128)(2,1)S(1)} %copy.31) | data formatting | bytes 1966080 | tf_op jit(solution)/shard_map/reshape | solution.py:66
  4.6 19.3 %all-to-all-start = ((bf16[64,1,15,512]{3,2,1,0:T(8,128)(2,1)}), bf16[64,1,15,512]{3,2,1,0:T(8,128)(2,1)S(1)}, u32[]{:S(2)}, u32[]{:S(2)}) async-start(bf16[64,1,15,512]{3,2,1,0:T(8,128)(2,1)} %reshape.152), calls=%async_computation | async-start | bytes 2097152 | tf_op jit(solution)/shard_map/all_to_all | solution.py:67
  23.9 0.0 copy-done
  23.9 27.1 %all-to-all-done = bf16[64,1,15,512]{3,2,1,0:T(8,128)(2,1)S(1)} async-done(((bf16[64,1,15,512]{3,2,1,0:T(8,128)(2,1)}), bf16[64,1,15,512]{3,2,1,0:T(8,128)(2,1)S(1)}, u32[]{:S(2)}, u32[]{:S(2)}) %all-to-all-start) | async-done | bytes 983072 | tf_op jit(solution)/shard_map/all_to_all | solution.py:67
  51.0 0.3 all_to_all.9
  51.3 0.7 multiply_reduce_fusion
  52.0 0.7 fusion.1
  52.7 1.1 %fusion.11 = (f32[128]{0:T(128)S(1)}, f32[960]{0:T(1024)S(1)}) fusion(bf16[1,1,960,512]{3,2,1,0:T(8,128)(2,1)S(1)} %all_to_all.9, f32[128]{0:T(128)S(1)} %dynamic-slice_bitcast_fusion, f32[960]{0:T(1024)S(1)} %fusion.1, f32[960]{0:T(1024)S(1)} %get-tuple-element.9, f32[960,960]{0,1:T(8,128)S(1)} %get-tuple-element.10), kind=kOutput, calls=%fused_computation.22 | convolution fusion | flops 240597952 | bytes 4436736 | tf_op jit(solution)/shard_map/vmap(vmap())/dot_general | solution.py:27
  53.8 0.9 convolution_convert_fusion.1
  54.8 1.1 %multiply_convert_fusion = bf16[960,960]{0,1:T(8,128)(2,1)S(1)} fusion(f32[960]{0:T(1024)S(1)} %get-tuple-element.5, bf16[1,1,960,512]{3,2,1,0:T(8,128)(2,1)S(1)} %all_to_all.9, f32[128]{0:T(128)S(1)} %dynamic-slice_bitcast_fusion, f32[960]{0:T(1024)S(1)} %fusion.1, f32[960]{0:T(1024)S(1)} %get-tuple-element.9, f32[960,960]{0,1:T(8,128)S(1)} %get-tuple-element.10), kind=kOutput, calls=%fused_computation | convolution fusion | flops 241827840 | bytes 6279680 | tf_op jit(solution)/shard_map/vmap(vmap())/dot_general | solution.py:31
  55.9 0.7 fusion.4
  56.6 0.8 fusion.3
  57.3 0.1 stack.11
  57.4 0.1 stack.9
  57.5 0.1 stack.10
  57.6 0.2 maximum_bitcast_fusion
  57.8 1.0 copy.25
  58.8 11.7 %all-to-all-start.1 = ((bf16[1,1,64,3,15,128]{5,4,0,1,3,2:T(8,128)(2,1)}), bf16[1,1,64,3,15,128]{5,4,0,1,3,2:T(8,128)(2,1)S(1)}, u32[]{:S(2)}, u32[]{:S(2)}) async-start(bf16[1,1,64,3,15,128]{5,4,0,1,3,2:T(8,128)(2,1)} %copy.25), calls=%async_computation.1 | async-start | bytes 1572864 | tf_op jit(solution)/shard_map/all_to_all | solution.py:82
  70.6 29.1 %psum.7 = f32[1,128]{1,0:T(1,128)} all-reduce(f32[1,128]{1,0:T(1,128)S(1)} %bitcast.83), channel_id=1, replica_groups=mesh['frame'=8,'space'=64] {'frame'}, use_global_device_ids=true, to_apply=%region_4.0 | all-reduce | flops 128 | bytes 1024 | tf_op jit(solution)/shard_map/psum | solution.py:87
  99.7 0.0 all-to-all-done.1
  99.7 0.1 slice_bitcast_fusion
  99.8 0.1 copy.28
  99.9 0.8 reshape.149
  100.7 0.1 copy.27
  100.8 0.8 reshape.148
  101.6 0.1 copy.26
  101.6 0.8 reshape.147
  (2 shorter events, 0.0 us)
Async XLA Ops:
  2.0 21.9 %copy-start = (f32[8,1024]{1,0:T(8,128)S(1)}, f32[8,1024]{1,0:T(8,128)}, u32[]{:S(2)}) copy-start(f32[8,1024]{1,0:T(8,128)} %param.9) | copy-start | bytes 98308
  4.6 46.4 %all-to-all-start = ((bf16[64,1,15,512]{3,2,1,0:T(8,128)(2,1)}), bf16[64,1,15,512]{3,2,1,0:T(8,128)(2,1)S(1)}, u32[]{:S(2)}, u32[]{:S(2)}) async-start(bf16[64,1,15,512]{3,2,1,0:T(8,128)(2,1)} %reshape.152), calls=%async_computation | async-start | bytes 2097152 | tf_op jit(solution)/shard_map/all_to_all | solution.py:67
  58.8 40.9 %all-to-all-start.1 = ((bf16[1,1,64,3,15,128]{5,4,0,1,3,2:T(8,128)(2,1)}), bf16[1,1,64,3,15,128]{5,4,0,1,3,2:T(8,128)(2,1)S(1)}, u32[]{:S(2)}, u32[]{:S(2)}) async-start(bf16[1,1,64,3,15,128]{5,4,0,1,3,2:T(8,128)(2,1)} %copy.25), calls=%async_computation.1 | async-start | bytes 1572864 | tf_op jit(solution)/shard_map/all_to_all | solution.py:82

commit v6 on v5

--- a/solution.py
+++ b/solution.py
@@ -63,10 +63,10 @@
     joined = joined.reshape(frames_local, pixels_local, clip_count, 4, head_count, DH)
     picker = jnp.eye(clip_count, dtype=joined.dtype)
     stacked = jnp.einsum("fibahd,bc->chfiad", joined, picker, preferred_element_type=jnp.float32)
-    stacked = stacked.astype(joined.dtype).reshape(pair_count, frames_local, pixels_local, 4 * DH)
+    stacked = stacked.astype(joined.dtype).reshape(pair_count, frames_local, pixels_local, 4, DH)
     gathered = lax.all_to_all(stacked, "space", split_axis=0, concat_axis=2, tiled=True)
     query_all, key_all, value_all, upstream_all = (
-        jnp.transpose(gathered[:, :, :, part * DH:(part + 1) * DH], (1, 2, 0, 3)) for part in range(4)
+        jnp.transpose(gathered[:, :, :, part, :], (1, 2, 0, 3)) for part in range(4)
     )
     gate_rows = lax.dynamic_slice_in_dim(
         gate_vec.reshape(pair_count, DH), lax.axis_index("space") * pairs_local, pairs_local, 0

time: 103 us -> 102 us (level)
    slice x0 -> x1, local copies, waits for them, and re-layouts: none -> 1.43 us  [local(): gathered[:, :, :, part, :]]
    reshape x2 -> x1, local copies, waits for them, and re-layouts: 2.13 us -> 1.72 us  [local(): stacked.astype(joined.dtype)]
where the time goes in v6:
time: 102 us
  starting transfers between devices  30.4 us (30%)
  blocking collectives  29.1 us (29%)
  waiting for transfers between devices  26.3 us (26%)
  local copies, waits for them, and re-layouts  7.47 us (7%)
  matrix products  5.76 us (6%)
  other arithmetic  2.25 us (2%)
    psum x1, blocking collectives, local(): grad_gate = lax.psum(pair_terms, 'frame')  29.1 us
    all_to_all x1, waiting for transfers between devices, local(): lax.all_to_all(stacked, 'space', split_axis=0, concat_axis=2, tiled=True)  26.3 us
    all_to_all x1, starting transfers between devices, local(): lax.all_to_all(stacked, 'space', split_axis=0, concat_axis=2, tiled=True)  19.3 us
    all_to_all x1, starting transfers between devices, local(): lax.all_to_all(grads, 'space', split_axis=2, concat_axis=0, tiled=True)  11.1 us
    reshape x3, local copies, waits for them, and re-layouts, by_width(): return tensor.reshape(frames_local, pixels_local, clip_count, channels)  2.4 us
  transfers between devices with their start and end apart: 2, of which 1 were waited for; matrix products, arithmetic and copies ran while one was open for 0% of the time, Pallas kernels for 0%

profile of v6, /device:TPU:6, one launch (start us, length us, event | category | flops | bytes accessed | tf_op | source)
XLA Modules:
  0.0 102.1 jit_solution(13745755834475099445)
XLA Ops:
  0.6 1.4 %pad_maximum_fusion = bf16[1,15,8,4096]{3,2,1,0:T(8,128)(2,1)S(1)} fusion(bf16[1,15,8,1024]{3,2,1,0:T(8,128)(2,1)} %param.8, bf16[1,15,8,1024]{3,2,1,0:T(8,128)(2,1)} %param.7, bf16[1,15,8,1024]{3,2,1,0:T(8,128)(2,1)} %param.6, bf16[1,15,8,1024]{3,2,1,0:T(8,128)(2,1)} %param.5), kind=kLoop, calls=%fused_computation.12 | loop fusion | flops 3932160 | bytes 1966080 | tf_op jit(solution)/shard_map/concatenate | solution.py:62
  2.0 0.0 copy-start
  2.0 0.4 fusion.2
  2.4 0.3 copy.72
  2.7 1.7 %copy.25 = bf16[64,1,15,4,128]{4,3,2,1,0:T(4,128)(2,1)} copy(bf16[64,1,15,4,128]{4,0,3,2,1:T(8,128)(2,1)S(1)} %bitcast.89) | data formatting | bytes 1966080 | tf_op jit(solution)/shard_map/reshape | solution.py:66
  4.4 19.3 %all-to-all-start = ((bf16[64,1,15,4,128]{4,3,2,1,0:T(4,128)(2,1)}), bf16[64,1,15,4,128]{4,3,2,1,0:T(4,128)(2,1)S(1)}, u32[]{:S(2)}, u32[]{:S(2)}) async-start(bf16[64,1,15,4,128]{4,3,2,1,0:T(4,128)(2,1)} %copy.25), calls=%async_computation | async-start | bytes 1966080 | tf_op jit(solution)/shard_map/all_to_all | solution.py:67
  23.7 0.0 copy-done
  23.8 26.3 %all-to-all-done = bf16[64,1,15,4,128]{4,3,2,1,0:T(4,128)(2,1)S(1)} async-done(((bf16[64,1,15,4,128]{4,3,2,1,0:T(4,128)(2,1)}), bf16[64,1,15,4,128]{4,3,2,1,0:T(4,128)(2,1)S(1)}, u32[]{:S(2)}, u32[]{:S(2)}) %all-to-all-start) | async-done | bytes 983072 | tf_op jit(solution)/shard_map/all_to_all | solution.py:67
  50.1 1.4 %fusion.34 = (bf16[1,1,960,1,128]{4,3,2,1,0:T(2,128)(2,1)S(1)}, bf16[1,1,960,1,128]{4,3,2,1,0:T(2,128)(2,1)S(1)}, bf16[1,1,960,1,128]{4,3,2,1,0:T(2,128)(2,1)S(1)}, bf16[1,1,960,1,128]{4,3,2,1,0:T(2,128)(2,1)S(1)}) fusion(bf16[1,1,960,4,128]{4,3,2,1,0:T(4,128)(2,1)S(1)} %bitcast.88), kind=kLoop, calls=%fused_computation.47 | loop fusion | bytes 1966080 | tf_op jit(solution)/shard_map/slice | solution.py:69
  51.5 0.7 multiply_reduce_fusion
  52.2 0.7 fusion.1
  52.9 1.2 %fusion.11 = (f32[128]{0:T(128)S(1)}, f32[960]{0:T(1024)S(1)}, bf16[1,1,960,1,128]{4,2,3,1,0:T(8,128)(2,1)S(1)}) fusion(f32[128]{0:T(128)S(1)} %dynamic-slice_bitcast_fusion, bf16[1,1,960,1,128]{4,3,2,1,0:T(2,128)(2,1)S(1)} %get-tuple-element.7, bf16[1,1,960,1,128]{4,3,2,1,0:T(2,128)(2,1)S(1)} %get-tuple-element.8, f32[960]{0:T(1024)S(1)} %fusion.1, ...), kind=kOutput, calls=%fused_computation.23 | convolution fusion | flops 240597952 | bytes 4436224 | tf_op jit(solution)/shard_map/vmap(vmap())/dot_general | solution.py:27
  54.1 1.2 %multiply_convert_fusion = bf16[960,960]{0,1:T(8,128)(2,1)S(1)} fusion(f32[960]{0:T(1024)S(1)} %get-tuple-element.5, bf16[1,1,960,1,128]{4,2,3,1,0:T(8,128)(2,1)S(1)} %get-tuple-element.6, f32[128]{0:T(128)S(1)} %dynamic-slice_bitcast_fusion, bf16[1,1,960,1,128]{4,3,2,1,0:T(2,128)(2,1)S(1)} %get-tuple-element.8, f32[960]{0:T(1024)S(1)} %fusion.1, ...), kind=kOutput, calls=%fused_computation | convolution fusion | flops 241827840 | bytes 6033152 | tf_op jit(solution)/shard_map/vmap(vmap())/dot_general | solution.py:31
  55.2 0.8 fusion.3
  56.0 0.7 fusion.4
  56.7 0.9 convolution_convert_fusion.1
  57.6 0.1 stack.9
  57.7 0.1 stack.10
  57.8 0.1 stack.11
  57.9 0.2 maximum_bitcast_fusion
  58.1 1.0 copy.28
  59.1 11.1 %all-to-all-start.1 = ((bf16[1,1,64,3,15,128]{5,4,0,1,3,2:T(8,128)(2,1)}), bf16[1,1,64,3,15,128]{5,4,0,1,3,2:T(8,128)(2,1)S(1)}, u32[]{:S(2)}, u32[]{:S(2)}) async-start(bf16[1,1,64,3,15,128]{5,4,0,1,3,2:T(8,128)(2,1)} %copy.28), calls=%async_computation.1 | async-start | bytes 1572864 | tf_op jit(solution)/shard_map/all_to_all | solution.py:82
  70.2 29.1 %psum.7 = f32[1,128]{1,0:T(1,128)} all-reduce(f32[1,128]{1,0:T(1,128)S(1)} %bitcast.92), channel_id=1, replica_groups=mesh['frame'=8,'space'=64] {'frame'}, use_global_device_ids=true, to_apply=%region_4.0 | all-reduce | flops 128 | bytes 1024 | tf_op jit(solution)/shard_map/psum | solution.py:87
  99.3 0.0 all-to-all-done.1
  99.3 0.1 slice_bitcast_fusion
  99.4 0.1 copy.29
  99.5 0.8 reshape.164
  100.3 0.1 copy.30
  100.4 0.8 reshape.165
  101.2 0.1 copy.31
  101.3 0.8 reshape.166
  (2 shorter events, 0.0 us)
Async XLA Ops:
  2.0 21.7 %copy-start = (f32[8,1024]{1,0:T(8,128)S(1)}, f32[8,1024]{1,0:T(8,128)}, u32[]{:S(2)}) copy-start(f32[8,1024]{1,0:T(8,128)} %param.9) | copy-start | bytes 98308
  4.4 45.6 %all-to-all-start = ((bf16[64,1,15,4,128]{4,3,2,1,0:T(4,128)(2,1)}), bf16[64,1,15,4,128]{4,3,2,1,0:T(4,128)(2,1)S(1)}, u32[]{:S(2)}, u32[]{:S(2)}) async-start(bf16[64,1,15,4,128]{4,3,2,1,0:T(4,128)(2,1)} %copy.25), calls=%async_computation | async-start | bytes 1966080 | tf_op jit(solution)/shard_map/all_to_all | solution.py:67
  59.1 40.2 %all-to-all-start.1 = ((bf16[1,1,64,3,15,128]{5,4,0,1,3,2:T(8,128)(2,1)}), bf16[1,1,64,3,15,128]{5,4,0,1,3,2:T(8,128)(2,1)S(1)}, u32[]{:S(2)}, u32[]{:S(2)}) async-start(bf16[1,1,64,3,15,128]{5,4,0,1,3,2:T(8,128)(2,1)} %copy.28), calls=%async_computation.1 | async-start | bytes 1572864 | tf_op jit(solution)/shard_map/all_to_all | solution.py:82

commit v7 on v6

--- a/solution.py
+++ b/solution.py
@@ -65,9 +65,10 @@
     stacked = jnp.einsum("fibahd,bc->chfiad", joined, picker, preferred_element_type=jnp.float32)
     stacked = stacked.astype(joined.dtype).reshape(pair_count, frames_local, pixels_local, 4, DH)
     gathered = lax.all_to_all(stacked, "space", split_axis=0, concat_axis=2, tiled=True)
-    query_all, key_all, value_all, upstream_all = (
-        jnp.transpose(gathered[:, :, :, part, :], (1, 2, 0, 3)) for part in range(4)
-    )
+    splitter = jnp.eye(4, dtype=gathered.dtype)
+    split_all = jnp.einsum("pfrad,ac->cfrpd", gathered, splitter, preferred_element_type=jnp.float32)
+    split_all = split_all.astype(gathered.dtype)
+    query_all, key_all, value_all, upstream_all = (split_all[part] for part in range(4))
     gate_rows = lax.dynamic_slice_in_dim(
         gate_vec.reshape(pair_count, DH), lax.axis_index("space") * pairs_local, pairs_local, 0
     )

time: 102 us -> 104 us (1.020)
  other arithmetic: 2.25 us -> 4.27 us
  local copies, waits for them, and re-layouts: 7.47 us -> 6.04 us
    slice x1 -> x0, local copies, waits for them, and re-layouts: 1.43 us -> none  [local(): gathered[:, :, :, part, :]]
    slice x0 -> x1, other arithmetic: none -> 1.39 us  [local(): split_all[part]]
where the time goes in v7:
time: 104 us; the launch traced here: 103 us
  starting transfers between devices  30.4 us (29%)
  blocking collectives  29.1 us (28%)
  waiting for transfers between devices  26.3 us (25%)
  matrix products  6.41 us (6%)
  local copies, waits for them, and re-layouts  6.04 us (6%)
  other arithmetic  4.27 us (4%)
    psum x1, blocking collectives, local(): grad_gate = lax.psum(pair_terms, 'frame')  29.1 us
    all_to_all x1, waiting for transfers between devices, local(): lax.all_to_all(stacked, 'space', split_axis=0, concat_axis=2, tiled=True)  26.3 us
    all_to_all x1, starting transfers between devices, local(): lax.all_to_all(stacked, 'space', split_axis=0, concat_axis=2, tiled=True)  19.3 us
    all_to_all x1, starting transfers between devices, local(): lax.all_to_all(grads, 'space', split_axis=2, concat_axis=0, tiled=True)  11.1 us
    reshape x3, local copies, waits for them, and re-layouts, by_width(): return tensor.reshape(frames_local, pixels_local, clip_count, channels)  2.4 us
  transfers between devices with their start and end apart: 2, of which 1 were waited for; matrix products, arithmetic and copies ran while one was open for 0% of the time, Pallas kernels for 0%

profile of v7, /device:TPU:6, one launch (start us, length us, event | category | flops | bytes accessed | tf_op | source)
XLA Modules:
  0.0 103.3 jit_solution(10731853609661784038)
XLA Ops:
  0.6 1.4 %pad_maximum_fusion = bf16[1,15,8,4096]{3,2,1,0:T(8,128)(2,1)S(1)} fusion(bf16[1,15,8,1024]{3,2,1,0:T(8,128)(2,1)} %param.8, bf16[1,15,8,1024]{3,2,1,0:T(8,128)(2,1)} %param.7, bf16[1,15,8,1024]{3,2,1,0:T(8,128)(2,1)} %param.6, bf16[1,15,8,1024]{3,2,1,0:T(8,128)(2,1)} %param.5), kind=kLoop, calls=%fused_computation.13 | loop fusion | flops 3932160 | bytes 1966080 | tf_op jit(solution)/shard_map/concatenate | solution.py:62
  2.0 0.0 copy-start
  2.0 0.4 fusion.2
  2.4 0.3 copy.72
  2.7 1.7 %copy.23 = bf16[64,1,15,4,128]{4,3,2,1,0:T(4,128)(2,1)} copy(bf16[64,1,15,4,128]{4,0,3,2,1:T(8,128)(2,1)S(1)} %bitcast.81) | data formatting | bytes 1966080 | tf_op jit(solution)/shard_map/reshape | solution.py:66
  4.4 19.3 %all-to-all-start = ((bf16[64,1,15,4,128]{4,3,2,1,0:T(4,128)(2,1)}), bf16[64,1,15,4,128]{4,3,2,1,0:T(4,128)(2,1)S(1)}, u32[]{:S(2)}, u32[]{:S(2)}) async-start(bf16[64,1,15,4,128]{4,3,2,1,0:T(4,128)(2,1)} %copy.23), calls=%async_computation | async-start | bytes 1966080 | tf_op jit(solution)/shard_map/all_to_all | solution.py:67
  23.7 0.0 copy-done
  23.8 26.3 %all-to-all-done = bf16[64,1,15,4,128]{4,3,2,1,0:T(4,128)(2,1)S(1)} async-done(((bf16[64,1,15,4,128]{4,3,2,1,0:T(4,128)(2,1)}), bf16[64,1,15,4,128]{4,3,2,1,0:T(4,128)(2,1)S(1)}, u32[]{:S(2)}, u32[]{:S(2)}) %all-to-all-start) | async-done | bytes 983072 | tf_op jit(solution)/shard_map/all_to_all | solution.py:67
  50.1 0.7 convolution_convert_fusion.1
  50.7 1.4 %fusion.29 = (bf16[1,960,128]{2,0,1:T(2,128)(2,1)S(1)}, f32[1,960,128]{2,0,1:T(1,128)S(1)}, bf16[1,960,128]{2,0,1:T(2,128)(2,1)S(1)}, bf16[1,960,128]{2,0,1:T(2,128)(2,1)S(1)}) fusion(bf16[4,960,128]{2,0,1:T(4,128)(2,1)S(1)} %convolution_convert_fusion.1), kind=kLoop, calls=%fused_computation.47 | loop fusion | flops 122880 | bytes 2211840 | tf_op jit(solution)/shard_map/slice | solution.py:71
  52.1 0.6 multiply_convert_fusion.2
  52.8 0.7 multiply_reduce_fusion
  53.5 0.7 fusion.1
  54.1 0.9 convolution_convert_fusion.2
  55.0 1.2 %multiply_reduce_fusion.1 = (f32[128]{0:T(128)S(1)}, f32[960]{0:T(1024)S(1)}) fusion(f32[960,128]{1,0:T(8,128)S(1)} %bitcast.85, f32[128]{0:T(128)S(1)} %dynamic-slice_bitcast_fusion, bf16[1,960,128]{2,0,1:T(2,128)(2,1)S(1)} %get-tuple-element.6, f32[960]{0:T(1024)S(1)} %fusion.1, f32[960]{0:T(1024)S(1)} %get-tuple-element.13, ...), kind=kOutput, calls=%fused_computation.20 | convolution fusion | flops 240475072 | bytes 4436224 | tf_op jit(solution)/shard_map/vmap(vmap())/dot_general | solution.py:27
  56.2 1.2 %multiply_convert_fusion = bf16[960,960]{0,1:T(8,128)(2,1)S(1)} fusion(f32[960]{0:T(1024)S(1)} %get-tuple-element.5, bf16[1,960,128]{2,0,1:T(2,128)(2,1)S(1)} %multiply_convert_fusion.2, bf16[1,960,128]{2,0,1:T(2,128)(2,1)S(1)} %get-tuple-element.6, f32[960]{0:T(1024)S(1)} %fusion.1, f32[960]{0:T(1024)S(1)} %get-tuple-element.13, ...), kind=kOutput, calls=%fused_computation | convolution fusion | flops 241459200 | bytes 6032640 | tf_op jit(solution)/shard_map/vmap(vmap())/dot_general | solution.py:31
  57.4 0.7 fusion.4
  58.1 0.8 fusion.3
  58.8 0.1 stack.9
  58.9 0.1 stack.10
  59.0 0.1 stack.11
  59.1 0.2 maximum_bitcast_fusion
  59.3 1.0 copy.25
  60.3 11.1 %all-to-all-start.1 = ((bf16[1,1,64,3,15,128]{5,4,0,1,3,2:T(8,128)(2,1)}), bf16[1,1,64,3,15,128]{5,4,0,1,3,2:T(8,128)(2,1)S(1)}, u32[]{:S(2)}, u32[]{:S(2)}) async-start(bf16[1,1,64,3,15,128]{5,4,0,1,3,2:T(8,128)(2,1)} %copy.25), calls=%async_computation.1 | async-start | bytes 1572864 | tf_op jit(solution)/shard_map/all_to_all | solution.py:83
  71.5 29.1 %psum.7 = f32[1,128]{1,0:T(1,128)} all-reduce(f32[1,128]{1,0:T(1,128)S(1)} %bitcast.86), channel_id=1, replica_groups=mesh['frame'=8,'space'=64] {'frame'}, use_global_device_ids=true, to_apply=%region_4.0 | all-reduce | flops 128 | bytes 1024 | tf_op jit(solution)/shard_map/psum | solution.py:88
  100.6 0.0 all-to-all-done.1
  100.6 0.1 slice_bitcast_fusion
  100.7 0.1 copy.28
  100.8 0.8 reshape.185
  101.6 0.1 copy.27
  101.7 0.8 reshape.184
  102.5 0.1 copy.26
  102.5 0.8 reshape.183
  (2 shorter events, 0.0 us)
Async XLA Ops:
  2.0 21.7 %copy-start = (f32[8,1024]{1,0:T(8,128)S(1)}, f32[8,1024]{1,0:T(8,128)}, u32[]{:S(2)}) copy-start(f32[8,1024]{1,0:T(8,128)} %param.9) | copy-start | bytes 98308
  4.4 45.6 %all-to-all-start = ((bf16[64,1,15,4,128]{4,3,2,1,0:T(4,128)(2,1)}), bf16[64,1,15,4,128]{4,3,2,1,0:T(4,128)(2,1)S(1)}, u32[]{:S(2)}, u32[]{:S(2)}) async-start(bf16[64,1,15,4,128]{4,3,2,1,0:T(4,128)(2,1)} %copy.23), calls=%async_computation | async-start | bytes 1966080 | tf_op jit(solution)/shard_map/all_to_all | solution.py:67
  60.3 40.2 %all-to-all-start.1 = ((bf16[1,1,64,3,15,128]{5,4,0,1,3,2:T(8,128)(2,1)}), bf16[1,1,64,3,15,128]{5,4,0,1,3,2:T(8,128)(2,1)S(1)}, u32[]{:S(2)}, u32[]{:S(2)}) async-start(bf16[1,1,64,3,15,128]{5,4,0,1,3,2:T(8,128)(2,1)} %copy.25), calls=%async_computation.1 | async-start | bytes 1572864 | tf_op jit(solution)/shard_map/all_to_all | solution.py:83
